TPU v7x, 128 devices: a whole 4x4x4 slice. The times are simulated.
128 devices in a mesh: outer: 8 (over z, core), inner: 16 (over x, y).
Axes of the slice: x: 4, y: 4, z: 4, core: 2. Of those that a mesh axis runs over, the one named last changes fastest.
Arguments:
- child_update: float32 [8, 2048, 2048], P('outer', 'inner'), may hold values from -1 to 8, as said below
- block_map: int32 [2, 8, 16], replicated, may hold values from 0 to 23, as said below
- obs_design: bfloat16 [262144, 128], P(('outer', 'inner')), may hold values from -2 to 2
- obs_target: int32 [262144], P(('outer', 'inner')), may hold values from 0 to 47
Outputs:
- pivot_factor: float32 [2, 8, 1024, 1024], P(None, 'outer', 'inner')
- border_factor: float32 [2, 8, 2048, 1024], P(None, 'outer', 'inner')
- top_update: float32 [8, 2048, 2048], P('outer', 'inner')
Inputs may be any that keep to these rules, and one draw needn't show every extreme that they name: `child_update`: each group's matrix is symmetric and positive definite. `block_map`: entry [l, g] names distinct parent blocks for the blocks of one child; groups under the same child hold equal entries; the two children of a parent together name every parent block.
All inputs are finite; a program needn't handle non-finite values.
Results may differ from a plain program's by a relative error of at most 0.0003.
Values sent between devices are 32-bit elements; how exact they have to be, the bound alone decides.
No kernel may reach another device: no remote copies, remote signals or barrier semaphores. Data moves between devices by JAX's collectives and lax.ppermute only.
A program may use at most 128 MiB of HBM per device.

v0:
```python
import math

import jax
import jax.numpy as jnp
from jax import lax
from jax.sharding import PartitionSpec as P

S = 1024
B = 2048
BLK = 128
LEVELS = 2


HIGHEST = lax.Precision.HIGHEST


def partner_2(block, axis, bit):
    count = lax.axis_size(axis)
    route = []
    for low in range(count):
        high = low | 1 << bit
        if high != low and high < count:
            route += [(low, high), (high, low)]
    return lax.ppermute(block, axis, route)


def block_source(child_map, parent_count):
    child_count = child_map.shape[0]
    matches = child_map[:, None] == jnp.arange(parent_count, dtype=jnp.int32)[None, :]
    source = jnp.sum(
        jnp.where(matches, jnp.arange(child_count, dtype=jnp.int32)[:, None], 0), axis=0
    )
    present = jnp.any(matches, axis=0)
    return (source, present)


def parent_columns(child_rows, child_map, parent_count):
    row_count = child_rows.shape[0]
    child_count = child_map.shape[0]
    block_size = child_rows.shape[1] // child_count
    source, present = block_source(child_map, parent_count)
    blocks = child_rows.reshape(row_count, child_count, block_size)
    picked = jnp.take(blocks, source, axis=1)
    picked = jnp.where(present[None, :, None], picked, jnp.zeros_like(picked))
    return picked.reshape(row_count, parent_count * block_size)


def parent_rows(child_cols, child_map, parent_count):
    col_count = child_cols.shape[1]
    child_count = child_map.shape[0]
    block_size = child_cols.shape[0] // child_count
    source, present = block_source(child_map, parent_count)
    blocks = child_cols.reshape(child_count, block_size, col_count)
    picked = jnp.take(blocks, source, axis=0)
    picked = jnp.where(present[:, None, None], picked, jnp.zeros_like(picked))
    return picked.reshape(parent_count * block_size, col_count)


def owner_major(parent_cols, inner_count):
    row_count = parent_cols.shape[0]
    sep_part = parent_cols[:, :S].reshape(row_count, inner_count, S // inner_count)
    border_part = parent_cols[:, S:].reshape(row_count, inner_count, B // inner_count)
    return jnp.concatenate([sep_part, border_part], axis=2)


def blocked_cholesky(matrix, panel_size):
    order = matrix.shape[0]
    lower_factor = jnp.zeros_like(matrix)
    trailing = matrix
    inverse_list = []
    for panel_index in range(order // panel_size):
        first = panel_index * panel_size
        last = first + panel_size
        diagonal_block = trailing[first:last, first:last]
        panel_lower = jnp.linalg.cholesky(diagonal_block)
        identity = jnp.eye(panel_size, dtype=jnp.float32)
        inverse = jax.scipy.linalg.solve_triangular(panel_lower, identity, lower=True)
        inverse_list.append(inverse)
        lower_factor = lower_factor.at[first:last, first:last].set(panel_lower)
        if last < order:
            below = jnp.dot(
                trailing[last:, first:last],
                inverse.T,
                precision=HIGHEST,
                preferred_element_type=jnp.float32,
            )
            lower_factor = lower_factor.at[last:, first:last].set(below)
            update = jnp.dot(below, below.T, precision=HIGHEST, preferred_element_type=jnp.float32)
            trailing = trailing.at[last:, last:].add(-update)
    return (lower_factor, inverse_list)


def border_solve(rows_in, lower_factor, inverse_list, panel_size):
    solved = []
    for panel_index in range(len(inverse_list)):
        first = panel_index * panel_size
        pending = rows_in[:, first : first + panel_size]
        for earlier in range(panel_index):
            coupling = lower_factor[
                first : first + panel_size, earlier * panel_size : (earlier + 1) * panel_size
            ]
            pending = pending - jnp.dot(
                solved[earlier], coupling.T, precision=HIGHEST, preferred_element_type=jnp.float32
            )
        solved.append(
            jnp.dot(
                pending,
                inverse_list[panel_index].T,
                precision=HIGHEST,
                preferred_element_type=jnp.float32,
            )
        )
    return jnp.concatenate(solved, axis=1)


def shards(child_update, block_map, obs_design, obs_target):
    inner_count = lax.axis_size("inner")
    group_count = lax.axis_size("outer")
    group_index = lax.axis_index("outer")
    member = lax.axis_index("inner")
    parent_count = (S + B) // BLK
    sep_rows = S // inner_count
    sep_blocks = S // BLK
    panel_size = min(S, 256)
    front_total = sum((group_count >> level_index + 1 for level_index in range(LEVELS)))
    target_total = front_total * sep_blocks
    row_count = obs_design.shape[0]
    step_rows = math.gcd(row_count, 256)
    target_ids = jnp.arange(target_total, dtype=jnp.int32)

    def add_rows(block_index, running):
        design = lax.dynamic_slice_in_dim(obs_design, block_index * step_rows, step_rows, 0)
        labels = lax.dynamic_slice_in_dim(obs_target, block_index * step_rows, step_rows, 0)
        selector = (labels[:, None] == target_ids[None, :]).astype(jnp.bfloat16)
        spread = selector[:, :, None] * design[:, None, :]
        return running + jnp.einsum(
            "rtj,rk->tjk", spread, design, preferred_element_type=jnp.float32
        )

    gram_blocks = lax.fori_loop(
        0, row_count // step_rows, add_rows, jnp.zeros((target_total, BLK, BLK), jnp.float32)
    )
    per_front = gram_blocks.reshape(front_total, S, BLK)
    summed = lax.psum(per_front, ("outer", "inner"))
    obs_share = lax.dynamic_slice_in_dim(summed, member * sep_rows, sep_rows, 1)
    current = child_update[0]
    pivot_list = []
    border_list = []
    front_offset = 0
    block_start = member * sep_rows // BLK * BLK
    for level_index in range(LEVELS):
        partner = group_index ^ 1 << level_index
        level_maps = block_map[level_index]
        own_map = lax.dynamic_index_in_dim(level_maps, group_index, 0, keepdims=False)
        sib_map = lax.dynamic_index_in_dim(level_maps, partner, 0, keepdims=False)
        sibling = partner_2(current, "outer", level_index)
        outgoing = jnp.stack(
            [
                owner_major(parent_columns(current, own_map, parent_count), inner_count),
                owner_major(parent_columns(sibling, sib_map, parent_count), inner_count),
            ]
        )
        arrived = lax.all_to_all(outgoing, "inner", split_axis=2, concat_axis=1, tiled=True)
        own_cols = parent_rows(arrived[0, :, 0, :], own_map, parent_count)
        sib_cols = parent_rows(arrived[1, :, 0, :], sib_map, parent_count)
        front_rows = (own_cols + sib_cols).T
        front_slot = front_offset + (group_index >> level_index + 1)
        obs_rows = lax.dynamic_index_in_dim(obs_share, front_slot, 0, keepdims=False)
        sep_front = front_rows[:sep_rows]
        block_now = lax.dynamic_slice_in_dim(sep_front, block_start, BLK, 1)
        sep_front = lax.dynamic_update_slice_in_dim(sep_front, block_now + obs_rows, block_start, 1)
        front_offset = front_offset + (group_count >> level_index + 1)
        pivot_all = lax.all_gather(sep_front[:, :S], "inner", axis=0, tiled=True)
        pivot_lower, inverse_list = blocked_cholesky(pivot_all, panel_size)
        border_front = front_rows[sep_rows:]
        border_factor = border_solve(border_front[:, :S], pivot_lower, inverse_list, panel_size)
        product = jnp.einsum(
            "rs,cs->rc",
            border_factor,
            lax.all_gather(border_factor, "inner", axis=0, tiled=True),
            precision=HIGHEST,
            preferred_element_type=jnp.float32,
        )
        current = border_front[:, S:] - product
        pivot_list.append(lax.dynamic_slice_in_dim(pivot_lower, member * sep_rows, sep_rows, 0))
        border_list.append(border_factor)
    pivot_factor = jnp.stack(pivot_list)[:, None]
    border_out = jnp.stack(border_list)[:, None]
    return (pivot_factor, border_out, current[None])


def solution(mesh):
    in_specs = (P("outer", "inner", None), P(), P(("outer", "inner"), None), P(("outer", "inner")))
    out_specs = (
        P(None, "outer", "inner", None),
        P(None, "outer", "inner", None),
        P("outer", "inner", None),
    )
    return jax.shard_map(shards, mesh=mesh, in_specs=in_specs, out_specs=out_specs, check_vma=False)
```

profile of v0, /device:TPU:1, one launch (start us, length us, event | category | flops | bytes accessed | tf_op | source)
XLA Modules:
  0.0 1201.5 jit_solution(18319998247828135470)
XLA Ops:
  45.3 25.9 %while.50 = (s32[]{:T(128)}, f32[48,128,128]{2,1,0:T(8,128)S(1)}, s32[2048]{0:T(1024)}, bf16[2048,128]{1,0:T(8,128)(2,1)}, s32[]{:T(128)}, /*index=5*/s32[]{:T(128)}, s32[]{:T(128)}, s32[]{:T(128)}) while((s32[]{:T(128)}, f32[48,128,128]{2,1,0:T(8,128)S(1)}, s32[2048]{0:T(1024)}, bf16[2048,128]{1,0:T(8,128)(2,1)}, s32[]{:T(128)}, ...), condition=%wide.region_5.8_spmd.clone, body=%wide.region_4.7_spmd.clone.sunk | while | flops 405823488 | bytes 6737045 | solution.py:140
  73.1 13.7 %all-to-all-done = f32[2,128,16,192]{1,3,0,2:T(8,128)} async-done(((f32[2,128,16,192]{1,3,0,2:T(8,128)}), f32[2,128,16,192]{1,3,0,2:T(8,128)}, u32[]{:S(2)}, u32[]{:S(2)}) %all-to-all-start) | async-done | bytes 3145760 | tf_op jit(solution)/shard_map/all_to_all | solution.py:163
  97.9 133.3 %all-reduce.5.cloned.1.call-done = f32[6,1024,128]{2,1,0:T(8,128)} async-done(((f32[6,1024,128]{2,1,0:T(8,128)}), f32[6,1024,128]{2,1,0:T(8,128)}) %all-reduce.5.cloned.1.call-update) | async-done | bytes 3145744 | tf_op jit(solution)/shard_map/psum | solution.py:144
  233.0 50.5 %all-gather.5.cloned.1.call-done = f32[1024,1024]{1,0:T(8,128)} async-done(((f32[64,1024]{1,0:T(8,128)}), f32[1024,1024]{1,0:T(8,128)}) %all-gather.5.cloned.1.call-update) | async-done | bytes 4194320 | tf_op jit(solution)/shard_map/all_gather | solution.py:173
  326.1 19.7 %custom-call.27 = f32[2,128,128]{1,2,0:T(8,128)S(1)} custom-call(f32[2,128,128]{2,1,0:T(8,128)S(1)} %get-tuple-element.409), custom_call_target="InvertDiagBlocksLowerTriangular" | custom-call | tf_op jit(solution)/shard_map/jit(_solve_triangular)/triangular_solve | solution.py:77
  383.3 11.9 cholesky.433
  402.6 19.7 %custom-call.29 = f32[2,128,128]{1,2,0:T(8,128)S(1)} custom-call(f32[2,128,128]{2,1,0:T(8,128)S(1)} %get-tuple-element.410), custom_call_target="InvertDiagBlocksLowerTriangular" | custom-call | tf_op jit(solution)/shard_map/jit(_solve_triangular)/triangular_solve | solution.py:77
  450.3 12.1 %cholesky.467 = f32[128,128]{1,0:T(8,128)S(1)} custom-call(f32[128,128]{1,0:T(8,128)S(1)} %convolution_subtract_fusion.27), custom_call_target="Cholesky" | custom-call | tf_op jit(solution)/shard_map/jit(cholesky)/cholesky | solution.py:75
  469.8 19.7 %custom-call.31 = f32[2,128,128]{1,2,0:T(8,128)S(1)} custom-call(f32[2,128,128]{2,1,0:T(8,128)S(1)} %get-tuple-element.411), custom_call_target="InvertDiagBlocksLowerTriangular" | custom-call | tf_op jit(solution)/shard_map/jit(_solve_triangular)/triangular_solve | solution.py:77
  524.7 13.2 %cholesky.501 = f32[128,128]{1,0:T(8,128)} custom-call(f32[128,128]{1,0:T(8,128)} %convolution_subtract_fusion.26), custom_call_target="Cholesky" | custom-call | tf_op jit(solution)/shard_map/jit(cholesky)/cholesky | solution.py:75
  555.3 21.1 %custom-call.33 = f32[2,128,128]{1,2,0:T(8,128)} custom-call(f32[2,128,128]{2,1,0:T(8,128)} %get-tuple-element.412), custom_call_target="InvertDiagBlocksLowerTriangular" | custom-call | tf_op jit(solution)/shard_map/jit(_solve_triangular)/triangular_solve | solution.py:77
  586.5 70.3 %all-gather.7.cloned.1.call-done = f32[2048,1024]{1,0:T(8,128)} async-done(((f32[128,1024]{1,0:T(8,128)}), f32[2048,1024]{1,0:T(8,128)}) %all-gather.7.cloned.1.call-update) | async-done | bytes 8388624 | tf_op jit(solution)/shard_map/all_gather | solution.py:180
  656.8 11.9 convolution_subtract_fusion.1
  676.9 16.0 %collective-permute-done.1 = f32[128,2048]{1,0:T(8,128)} collective-permute-done((f32[128,2048]{1,0:T(8,128)}, f32[128,2048]{1,0:T(8,128)}, u32[]{:S(2)}, u32[]{:S(2)}) %collective-permute-start.1) | collective-permute-done | bytes 1048608 | tf_op jit(solution)/shard_map/ppermute | solution.py:24
  707.1 37.1 %all-to-all-done.1 = f32[2,128,16,192]{1,3,0,2:T(8,128)S(1)} async-done(((f32[2,128,16,192]{1,3,0,2:T(8,128)}), f32[2,128,16,192]{1,3,0,2:T(8,128)S(1)}, u32[]{:S(2)}, u32[]{:S(2)}) %all-to-all-start.1) | async-done | bytes 3145760 | tf_op jit(solution)/shard_map/all_to_all | solution.py:163
  754.8 55.1 %all-gather.9.cloned.1.call-done = f32[1024,1024]{1,0:T(8,128)} async-done(((f32[64,1024]{1,0:T(8,128)}), f32[1024,1024]{1,0:T(8,128)}) %all-gather.9.cloned.1.call-update) | async-done | bytes 4194320 | tf_op jit(solution)/shard_map/all_gather | solution.py:173
  852.5 19.7 %custom-call.35 = f32[2,128,128]{1,2,0:T(8,128)S(1)} custom-call(f32[2,128,128]{2,1,0:T(8,128)S(1)} %get-tuple-element.413), custom_call_target="InvertDiagBlocksLowerTriangular" | custom-call | tf_op jit(solution)/shard_map/jit(_solve_triangular)/triangular_solve | solution.py:77
  909.5 12.1 %cholesky.569 = f32[128,128]{1,0:T(8,128)S(1)} custom-call(f32[128,128]{1,0:T(8,128)S(1)} %convolution_subtract_fusion.24), custom_call_target="Cholesky" | custom-call | tf_op jit(solution)/shard_map/jit(cholesky)/cholesky | solution.py:75
  929.0 19.7 %custom-call.37 = f32[2,128,128]{1,2,0:T(8,128)S(1)} custom-call(f32[2,128,128]{2,1,0:T(8,128)S(1)} %get-tuple-element.414), custom_call_target="InvertDiagBlocksLowerTriangular" | custom-call | tf_op jit(solution)/shard_map/jit(_solve_triangular)/triangular_solve | solution.py:77
  996.0 19.7 %custom-call.39 = f32[2,128,128]{1,2,0:T(8,128)S(1)} custom-call(f32[2,128,128]{2,1,0:T(8,128)S(1)} %get-tuple-element.415), custom_call_target="InvertDiagBlocksLowerTriangular" | custom-call | tf_op jit(solution)/shard_map/jit(_solve_triangular)/triangular_solve | solution.py:77
  1050.9 13.2 %cholesky.637 = f32[128,128]{1,0:T(8,128)} custom-call(f32[128,128]{1,0:T(8,128)} %convolution_subtract_fusion.22), custom_call_target="Cholesky" | custom-call | tf_op jit(solution)/shard_map/jit(cholesky)/cholesky | solution.py:75
  1081.3 21.1 %custom-call.41 = f32[2,128,128]{1,2,0:T(8,128)} custom-call(f32[2,128,128]{2,1,0:T(8,128)} %get-tuple-element.416), custom_call_target="InvertDiagBlocksLowerTriangular" | custom-call | tf_op jit(solution)/shard_map/jit(_solve_triangular)/triangular_solve | solution.py:77
  1116.3 66.6 %all-gather.11.cloned.1.call-done = f32[2048,1024]{1,0:T(8,128)} async-done(((f32[128,1024]{1,0:T(8,128)}), f32[2048,1024]{1,0:T(8,128)}) %all-gather.11.cloned.1.call-update) | async-done | bytes 8388624 | tf_op jit(solution)/shard_map/all_gather | solution.py:180
  1182.9 11.9 fusion.10
  (425 shorter events, 520.3 us)
Async XLA Ops:
  9.7 12.5 %collective-permute-start = (f32[128,2048]{0,1:T(8,128)}, f32[128,2048]{0,1:T(8,128)}, u32[]{:S(2)}, u32[]{:S(2)}) collective-permute-start(f32[128,2048]{0,1:T(8,128)} %bitcast.8), channel_id=1, source_target_pairs={{0,16},{16,0},{32,48},{48,32},{64,80},{80,64},{96,112},{112,96},{1... | collective-permute-start | bytes 3145736 | tf_op jit(solution)/shard_map/ppermute | solution.py:24
  38.4 48.5 %all-to-all-start = ((f32[2,128,16,192]{1,3,0,2:T(8,128)}), f32[2,128,16,192]{1,3,0,2:T(8,128)}, u32[]{:S(2)}, u32[]{:S(2)}) async-start(f32[2,128,16,192]{1,3,0,2:T(8,128)} %pad_maximum_fusion), calls=%async_computation | async-start | bytes 6291456 | tf_op jit(solution)/shard_map/all_to_all | solution.py:163
  45.3 185.9 %all-reduce.5.cloned.1.call-start = ((), (), s32[]{:S(2)}) async-start(), calls=%async_computation.2 | async-start | bytes 6291456 | tf_op jit(solution)/shard_map/psum | solution.py:144
  71.3 1.7 copy-start
  73.0 210.5 %all-gather.5.cloned.1.call-start = ((), (), s32[]{:S(2)}) async-start(), calls=%async_computation.3 | async-start | bytes 4456448 | tf_op jit(solution)/shard_map/all_gather | solution.py:173
  232.7 424.1 %all-gather.7.cloned.1.call-start = ((), (), s32[]{:S(2)}) async-start(), calls=%async_computation.4 | async-start | bytes 8912896 | tf_op jit(solution)/shard_map/all_gather | solution.py:180
  356.2 2.3 copy-start.5
  360.1 63.1 %copy-start.8 = (f32[768,768]{0,1:T(8,128)S(1)}, f32[768,768]{0,1:T(8,128)}, u32[]{:S(2)}) copy-start(f32[768,768]{0,1:T(8,128)} %copy-done.7) | copy-start | bytes 7077892
  469.8 26.9 %copy-start.25 = (s32[2,2]{1,0:T(2,128)}, s32[2,2]{1,0:T(2,128)S(1)}, u32[]{:S(2)}) copy-start(s32[2,2]{1,0:T(2,128)S(1)} %get-tuple-element.1052) | copy-start | bytes 52
  492.7 50.4 %copy-start.2 = (f32[192,3072]{1,0:T(8,128)S(1)}, f32[192,3072]{1,0:T(8,128)}, u32[]{:S(2)}) copy-start(f32[192,3072]{1,0:T(8,128)} %copy-done.1) | copy-start | bytes 7077892
  538.8 2.6 copy-start.17
  540.0 9.9 copy-start.26
  576.3 5.7 copy-start.22
  668.7 24.2 %collective-permute-start.1 = (f32[128,2048]{1,0:T(8,128)}, f32[128,2048]{1,0:T(8,128)}, u32[]{:S(2)}, u32[]{:S(2)}) collective-permute-start(f32[128,2048]{1,0:T(8,128)} %convolution_subtract_fusion.1), channel_id=1, source_target_pairs={{0,32},{32,0},{16,48},{48,16},{64,96},{96,64},{80,112},{112,80},{1... | collective-permute-start | bytes 3145736 | tf_op jit(solution)/shard_map/ppermute | solution.py:24
  701.6 42.5 %all-to-all-start.1 = ((f32[2,128,16,192]{1,3,0,2:T(8,128)}), f32[2,128,16,192]{1,3,0,2:T(8,128)S(1)}, u32[]{:S(2)}, u32[]{:S(2)}) async-start(f32[2,128,16,192]{1,3,0,2:T(8,128)} %pad_maximum_fusion.1), calls=%async_computation.1 | async-start | bytes 6291456 | tf_op jit(solution)/shard_map/all_to_all | solution.py:163
  706.6 103.3 %all-gather.9.cloned.1.call-start = ((), (), s32[]{:S(2)}) async-start(), calls=%async_computation.5 | async-start | bytes 4456448 | tf_op jit(solution)/shard_map/all_gather | solution.py:173
  754.8 428.1 %all-gather.11.cloned.1.call-start = ((), (), s32[]{:S(2)}) async-start(), calls=%async_computation.6 | async-start | bytes 8912896 | tf_op jit(solution)/shard_map/all_gather | solution.py:180
  882.3 2.3 copy-start.6
  886.3 63.3 %copy-start.10 = (f32[768,768]{0,1:T(8,128)S(1)}, f32[768,768]{0,1:T(8,128)}, u32[]{:S(2)}) copy-start(f32[768,768]{0,1:T(8,128)} %copy-done.9) | copy-start | bytes 7077892
  1018.9 50.5 %copy-start.4 = (f32[192,3072]{1,0:T(8,128)S(1)}, f32[192,3072]{1,0:T(8,128)}, u32[]{:S(2)}) copy-start(f32[192,3072]{1,0:T(8,128)} %copy-done.3) | copy-start | bytes 7077892
  1065.0 2.7 copy-start.18
  1102.4 5.7 copy-start.21
  1110.8 4.4 copy-start.15
  1112.3 2.9 copy-start.16
  (12 other events, 13.4 us)
Sparse Core Ops, SparseCore 0:
  73.2 157.9 all-reduce.4
  233.9 49.5 all-gather.4
  586.4 70.3 all-gather.6
  754.9 54.9 all-gather.8
  1112.5 70.3 all-gather.10
where the time goes:
time: 1210 us; the launch traced here: 1200 us
  other arithmetic  489 us (40%)
  waiting for transfers between devices  443 us (37%)
  local copies, waits for them, and re-layouts  124 us (10%)
  matrix products  104 us (9%)
  between operations  25.9 us (2%)
  starting transfers between devices  15.3 us (1%)
    another operation x56, other arithmetic, blocked_cholesky(): panel_lower = jnp.linalg.cholesky(diagonal_block)  287 us
    another operation x17, other arithmetic, blocked_cholesky(): jax.scipy.linalg.solve_triangular(panel_lower, identity, lower=True)  167 us
    all_gather x2, waiting for transfers between devices, shards(): lax.all_gather(border_factor, 'inner', axis=0, tiled=True)  137 us
    psum x1, waiting for transfers between devices, shards(): summed = lax.psum(per_front, ('outer', 'inner'))  133 us
    all_gather x2, waiting for transfers between devices, shards(): pivot_all = lax.all_gather(sep_front[:, :S], 'inner', axis=0, tiled=True)  106 us
    all_to_all x2, waiting for transfers between devices, shards(): lax.all_to_all(outgoing, 'inner', split_axis=2, concat_axis=1, tiled=True)  50.8 us
    another operation x57, local copies, waits for them, and re-layouts, blocked_cholesky(): jax.scipy.linalg.solve_triangular(panel_lower, identity, lower=True)  35.4 us
  transfers between devices with their start and end apart: 9, of which 8 were waited for; matrix products, arithmetic and copies ran while one was open for 5% of the time, Pallas kernels for 0%

commit v1 on v0

--- a/solution.py
+++ b/solution.py
@@ -90,6 +90,29 @@
     return (lower_factor, inverse_list)
 
 
+def cholesky_inverse(matrix, base_size):
+    order = matrix.shape[0]
+    if order <= base_size:
+        lower = jnp.linalg.cholesky(matrix)
+        identity = jnp.eye(order, dtype=jnp.float32)
+        return (lower, jax.scipy.linalg.solve_triangular(lower, identity, lower=True))
+    half = order // 2
+    lower_11, inverse_11 = cholesky_inverse(matrix[:half, :half], base_size)
+    lower_21 = jnp.dot(matrix[half:, :half], inverse_11.T, precision=HIGHEST, preferred_element_type=jnp.float32)
+    schur = matrix[half:, half:] - jnp.dot(lower_21, lower_21.T, precision=HIGHEST, preferred_element_type=jnp.float32)
+    lower_22, inverse_22 = cholesky_inverse(schur, base_size)
+    inverse_21 = -jnp.dot(
+        inverse_22,
+        jnp.dot(lower_21, inverse_11, precision=HIGHEST, preferred_element_type=jnp.float32),
+        precision=HIGHEST,
+        preferred_element_type=jnp.float32,
+    )
+    zero = jnp.zeros((half, half), jnp.float32)
+    lower = jnp.block([[lower_11, zero], [lower_21, lower_22]])
+    inverse = jnp.block([[inverse_11, zero], [inverse_21, inverse_22]])
+    return (lower, inverse)
+
+
 def border_solve(rows_in, lower_factor, inverse_list, panel_size):
     solved = []
     for panel_index in range(len(inverse_list)):
@@ -141,8 +164,7 @@
         0, row_count // step_rows, add_rows, jnp.zeros((target_total, BLK, BLK), jnp.float32)
     )
     per_front = gram_blocks.reshape(front_total, S, BLK)
-    summed = lax.psum(per_front, ("outer", "inner"))
-    obs_share = lax.dynamic_slice_in_dim(summed, member * sep_rows, sep_rows, 1)
+    obs_share = lax.psum(lax.psum_scatter(per_front, "inner", scatter_dimension=1, tiled=True), "outer")
     current = child_update[0]
     pivot_list = []
     border_list = []
@@ -171,13 +193,17 @@
         sep_front = lax.dynamic_update_slice_in_dim(sep_front, block_now + obs_rows, block_start, 1)
         front_offset = front_offset + (group_count >> level_index + 1)
         pivot_all = lax.all_gather(sep_front[:, :S], "inner", axis=0, tiled=True)
-        pivot_lower, inverse_list = blocked_cholesky(pivot_all, panel_size)
         border_front = front_rows[sep_rows:]
-        border_factor = border_solve(border_front[:, :S], pivot_lower, inverse_list, panel_size)
+        coupling_all = lax.all_gather(border_front[:, :S], "inner", axis=0, tiled=True)
+        pivot_lower, pivot_inverse = cholesky_inverse(pivot_all, BLK)
+        border_all = jnp.dot(
+            coupling_all, pivot_inverse.T, precision=HIGHEST, preferred_element_type=jnp.float32
+        )
+        border_factor = lax.dynamic_slice_in_dim(border_all, member * (B // inner_count), B // inner_count, 0)
         product = jnp.einsum(
             "rs,cs->rc",
             border_factor,
-            lax.all_gather(border_factor, "inner", axis=0, tiled=True),
+            border_all,
             precision=HIGHEST,
             preferred_element_type=jnp.float32,
         )

time: 1210 us -> 1060 us (0.88)
  waiting for transfers between devices: 443 us -> 241 us
  matrix products: 104 us -> 169 us
  blocking collectives: 0 us -> 42.2 us
  other arithmetic: 489 us -> 460 us
    all_gather x2, waiting for transfers between devices: 137 us -> 0.01 us  [shards(): lax.all_gather(border_front[:, :S], 'inner', axis=0, tiled=True)]
    psum x1, waiting for transfers between devices: 133 us -> 58.8 us  [shards(): lax.psum(lax.psum_scatter(per_front, 'inner', scatter_dimension=1, tiled=...]
    dot_general x34 -> x60, matrix products: 73.1 us -> 144 us  [the longest x2 66.8 us: shards(): jnp.dot(coupling_all, pivot_inverse.T, precision=HIGHEST, preferred_eleme...]
    another operation x74 -> x81, other arithmetic: 455 us -> 407 us  [the longest x48 214 us: cholesky_inverse(): lower = jnp.linalg.cholesky(matrix)]
    all_to_all x0 -> x1, blocking collectives: none -> 42.2 us  [shards(): lax.all_to_all(outgoing, 'inner', split_axis=2, concat_axis=1, tiled=True)]
    reduce_scatter x0 -> x1, waiting for transfers between devices: none -> 39.4 us  [shards(): lax.psum_scatter(per_front, 'inner', scatter_dimension=1, tiled=True)]
    another operation x77 -> x10, local copies, waits for them, and re-layouts: 45.8 us -> 8.51 us  [the longest x8 6.59 us: cholesky_inverse(): jax.scipy.linalg.solve_triangular(lower, identity, lower=True)]
    all_gather x2, waiting for transfers between devices: 106 us -> 79.9 us  [shards(): pivot_all = lax.all_gather(sep_front[:, :S], 'inner', axis=0, tiled=True)]
  transfers between devices with their start and end apart: 9 -> 9, of which waited for: 8 -> 6; matrix products, arithmetic and copies ran while one was open for 5% -> 59% of each run, Pallas kernels for 0% -> 0%
where the time goes in v1:
time: 1060 us; the launch traced here: 1050 us
  other arithmetic  460 us (43%)
  waiting for transfers between devices  241 us (23%)
  matrix products  169 us (16%)
  local copies, waits for them, and re-layouts  113 us (11%)
  blocking collectives  42.2 us (4%)
  between operations  16.7 us (2%)
    another operation x48, other arithmetic, cholesky_inverse(): lower = jnp.linalg.cholesky(matrix)  214 us
    another operation x32, other arithmetic, cholesky_inverse(): jax.scipy.linalg.solve_triangular(lower, identity, lower=True)  192 us
    all_gather x2, waiting for transfers between devices, shards(): pivot_all = lax.all_gather(sep_front[:, :S], 'inner', axis=0, tiled=True)  79.9 us
    dot_general x2, matrix products, shards(): jnp.dot(coupling_all, pivot_inverse.T, precision=HIGHEST, preferred_eleme...  66.8 us
    psum x1, waiting for transfers between devices, shards(): lax.psum(lax.psum_scatter(per_front, 'inner', scatter_dimension=1, tiled=...  58.8 us
    all_to_all x1, waiting for transfers between devices, shards(): lax.all_to_all(outgoing, 'inner', split_axis=2, concat_axis=1, tiled=True)  46.6 us
    all_to_all x1, blocking collectives, shards(): lax.all_to_all(outgoing, 'inner', split_axis=2, concat_axis=1, tiled=True)  42.2 us
    reduce_scatter x1, waiting for transfers between devices, shards(): lax.psum_scatter(per_front, 'inner', scatter_dimension=1, tiled=True)  39.4 us
  transfers between devices with their start and end apart: 9, of which 6 were waited for; matrix products, arithmetic and copies ran while one was open for 59% of the time, Pallas kernels for 0%

profile of v1, /device:TPU:1, one launch (start us, length us, event | category | flops | bytes accessed | tf_op | source)
XLA Modules:
  0.0 1052.6 jit_solution(1851597873496397429)
XLA Ops:
  11.1 25.9 %while.14 = (s32[]{:T(128)}, f32[48,128,128]{2,1,0:T(8,128)S(1)}, s32[2048]{0:T(1024)}, bf16[2048,128]{1,0:T(8,128)(2,1)}, s32[]{:T(128)}, /*index=5*/s32[]{:T(128)}, s32[]{:T(128)}, s32[]{:T(128)}) while((s32[]{:T(128)}, f32[48,128,128]{2,1,0:T(8,128)S(1)}, s32[2048]{0:T(1024)}, bf16[2048,128]{1,0:T(8,128)(2,1)}, s32[]{:T(128)}, ...), condition=%wide.region_5.8_spmd.clone, body=%wide.region_4.7_spmd.clone.sunk | while | flops 405823488 | bytes 6737053 | solution.py:163
  64.3 46.6 %all-to-all-done = f32[2,128,16,192]{1,3,0,2:T(8,128)S(1)} async-done(((f32[2,128,16,192]{1,3,0,2:T(8,128)}), f32[2,128,16,192]{1,3,0,2:T(8,128)S(1)}, u32[]{:S(2)}, u32[]{:S(2)}) %all-to-all-start) | async-done | bytes 3145760 | tf_op jit(solution)/shard_map/all_to_all | solution.py:185
  115.6 39.4 %reduce-scatter.2.cloned.1.call-done = f32[6,64,128]{2,0,1:T(8,128)} async-done(((f32[6,1024,128]{2,0,1:T(8,128)}), f32[6,64,128]{2,0,1:T(8,128)}) %reduce-scatter.2.cloned.1.call-update) | async-done | bytes 196624 | tf_op jit(solution)/shard_map/reduce_scatter | solution.py:167
  158.0 58.8 %all-reduce.30.cloned.1.call-done = f32[6,64,128]{2,0,1:T(8,128)} async-done(((f32[6,64,128]{2,0,1:T(8,128)}), f32[6,64,128]{2,0,1:T(8,128)}) %all-reduce.30.cloned.1.call-update) | async-done | bytes 196624 | tf_op jit(solution)/shard_map/psum | solution.py:167
  221.2 50.5 %all-gather.5.cloned.1.call-done = f32[1024,1024]{1,0:T(8,128)} async-done(((f32[64,1024]{1,0:T(8,128)}), f32[1024,1024]{1,0:T(8,128)}) %all-gather.5.cloned.1.call-update) | async-done | bytes 4194320 | tf_op jit(solution)/shard_map/all_gather | solution.py:195
  273.7 11.7 %cholesky.254 = f32[128,128]{1,0:T(8,128)S(1)} custom-call(f32[128,128]{1,0:T(8,128)S(1)} %get-tuple-element.171), custom_call_target="Cholesky" | custom-call | tf_op jit(solution)/shard_map/jit(cholesky)/cholesky | solution.py:96
  299.0 11.7 %cholesky.265 = f32[128,128]{1,0:T(8,128)S(1)} custom-call(f32[128,128]{1,0:T(8,128)S(1)} %fusion.203), custom_call_target="Cholesky" | custom-call | tf_op jit(solution)/shard_map/jit(cholesky)/cholesky | solution.py:96
  351.3 12.1 %cholesky.287 = f32[128,128]{1,0:T(8,128)S(1)} custom-call(f32[128,128]{1,0:T(8,128)S(1)} %fusion.199), custom_call_target="Cholesky" | custom-call | tf_op jit(solution)/shard_map/jit(cholesky)/cholesky | solution.py:96
  391.9 12.7 %cholesky.298 = f32[128,128]{1,0:T(8,128)S(1)} custom-call(f32[128,128]{1,0:T(8,128)} %fusion.197), custom_call_target="Cholesky" | custom-call | tf_op jit(solution)/shard_map/jit(cholesky)/cholesky | solution.py:96
  425.3 13.2 %cholesky.309 = f32[128,128]{1,0:T(8,128)} custom-call(f32[128,128]{1,0:T(8,128)} %fusion.195), custom_call_target="Cholesky" | custom-call | tf_op jit(solution)/shard_map/jit(cholesky)/cholesky | solution.py:96
  467.7 13.5 %cholesky.320 = f32[128,128]{1,0:T(8,128)} custom-call(f32[128,128]{1,0:T(8,128)} %fusion.193), custom_call_target="Cholesky" | custom-call | tf_op jit(solution)/shard_map/jit(cholesky)/cholesky | solution.py:96
  504.6 13.2 %cholesky.331 = f32[128,128]{1,0:T(8,128)} custom-call(f32[128,128]{1,0:T(8,128)} %fusion.191), custom_call_target="Cholesky" | custom-call | tf_op jit(solution)/shard_map/jit(cholesky)/cholesky | solution.py:96
  547.2 36.0 %fusion.12 = f32[2048,1024]{1,0:T(8,128)S(1)} fusion(f32[2048,1024]{1,0:T(8,128)} %all-gather.7.cloned.1.call-done, f32[512,512]{1,0:T(8,128)S(1)} %copy-done.37, f32[128,128]{1,0:T(8,128)S(1)} %copy-done.85, f32[128,128]{1,0:T(8,128)} %copy-done.81, f32[128,256]{1,0:T(8,128)} %concatenate.310, f32[256,256]{1,0:T(8,128)} %copy-done.77, ...), kind=kOutput, calls=%fused_computation.29 | convolution fusion | flops 25778192384 | bytes 19922944 | tf_op jit(solution)/shard_map/dot_general | solution.py:199
  601.0 16.1 %collective-permute-done.1 = f32[128,2048]{1,0:T(8,128)} collective-permute-done((f32[128,2048]{1,0:T(8,128)}, f32[128,2048]{1,0:T(8,128)}, u32[]{:S(2)}, u32[]{:S(2)}) %collective-permute-start.1) | collective-permute-done | bytes 1048608 | tf_op jit(solution)/shard_map/ppermute | solution.py:24
  624.1 42.2 %all_to_all.30 = f32[2,128,16,192]{1,3,0,2:T(8,128)S(1)} all-to-all(f32[2,128,16,192]{1,3,0,2:T(8,128)S(1)} %pad_maximum_fusion.1), channel_id=1, replica_groups=mesh['outer'=8,'inner'=16] {'inner'}, dimensions={2} | all-to-all | bytes 6291456 | tf_op jit(solution)/shard_map/all_to_all | solution.py:185
  697.1 29.4 %all-gather.9.cloned.1.call-done = f32[1024,1024]{1,0:T(8,128)} async-done(((f32[64,1024]{1,0:T(8,128)}), f32[1024,1024]{1,0:T(8,128)}) %all-gather.9.cloned.1.call-update) | async-done | bytes 4194320 | tf_op jit(solution)/shard_map/all_gather | solution.py:195
  728.4 11.7 %cholesky.342 = f32[128,128]{1,0:T(8,128)S(1)} custom-call(f32[128,128]{1,0:T(8,128)S(1)} %get-tuple-element.169), custom_call_target="Cholesky" | custom-call | tf_op jit(solution)/shard_map/jit(cholesky)/cholesky | solution.py:96
  754.6 11.9 %cholesky.353 = f32[128,128]{1,0:T(8,128)S(1)} custom-call(f32[128,128]{1,0:T(8,128)S(1)} %fusion.187), custom_call_target="Cholesky" | custom-call | tf_op jit(solution)/shard_map/jit(cholesky)/cholesky | solution.py:96
  808.5 11.9 %cholesky.375 = f32[128,128]{1,0:T(8,128)S(1)} custom-call(f32[128,128]{1,0:T(8,128)S(1)} %fusion.183), custom_call_target="Cholesky" | custom-call | tf_op jit(solution)/shard_map/jit(cholesky)/cholesky | solution.py:96
  849.3 12.1 %cholesky.386 = f32[128,128]{1,0:T(8,128)S(1)} custom-call(f32[128,128]{1,0:T(8,128)S(1)} %fusion.181), custom_call_target="Cholesky" | custom-call | tf_op jit(solution)/shard_map/jit(cholesky)/cholesky | solution.py:96
  881.7 13.2 %cholesky.397 = f32[128,128]{1,0:T(8,128)} custom-call(f32[128,128]{1,0:T(8,128)} %fusion.179), custom_call_target="Cholesky" | custom-call | tf_op jit(solution)/shard_map/jit(cholesky)/cholesky | solution.py:96
  924.6 12.5 %cholesky.408 = f32[128,128]{1,0:T(8,128)S(1)} custom-call(f32[128,128]{1,0:T(8,128)} %fusion.177), custom_call_target="Cholesky" | custom-call | tf_op jit(solution)/shard_map/jit(cholesky)/cholesky | solution.py:96
  957.2 13.2 %cholesky.419 = f32[128,128]{1,0:T(8,128)} custom-call(f32[128,128]{1,0:T(8,128)} %fusion.175), custom_call_target="Cholesky" | custom-call | tf_op jit(solution)/shard_map/jit(cholesky)/cholesky | solution.py:96
  1003.9 30.8 %fusion.10 = f32[2048,1024]{1,0:T(8,128)S(1)} fusion(f32[2048,1024]{1,0:T(8,128)} %all-gather.11.cloned.1.call-done, f32[512,512]{1,0:T(8,128)S(1)} %copy-done.36, f32[128,128]{1,0:T(8,128)} %copy.496, f32[128,128]{1,0:T(8,128)} %copy-done.80, f32[128,256]{1,0:T(8,128)S(1)} %copy-done.67, f32[256,256]{1,0:T(8,128)} %copy-done.76, ...), kind=kOutput, calls=%fused_computation.23 | convolution fusion | flops 25778192384 | bytes 19922944 | tf_op jit(solution)/shard_map/dot_general | solution.py:199
  (551 shorter events, 511.1 us)
Async XLA Ops:
  7.2 147.8 %reduce-scatter.2.cloned.1.call-start = ((), (), s32[]{:S(2)}) async-start(), calls=%async_computation.3 | async-start | bytes 4456448 | tf_op jit(solution)/shard_map/reduce_scatter | solution.py:167
  9.7 38.6 %collective-permute-start = (f32[128,2048]{0,1:T(8,128)}, f32[128,2048]{0,1:T(8,128)}, u32[]{:S(2)}, u32[]{:S(2)}) collective-permute-start(f32[128,2048]{0,1:T(8,128)} %bitcast.8), channel_id=1, source_target_pairs={{0,16},{16,0},{32,48},{48,32},{64,80},{80,64},{96,112},{112,96},{1... | collective-permute-start | bytes 3145736 | tf_op jit(solution)/shard_map/ppermute | solution.py:24
  42.7 177.7 %copy-start.89 = (s32[24]{0:T(128)}, s32[24]{0:T(128)S(1)}, u32[]{:S(2)}) copy-start(s32[24]{0:T(128)S(1)} %get-tuple-element.186) | copy-start | bytes 292
  57.3 53.5 %all-to-all-start = ((f32[2,128,16,192]{1,3,0,2:T(8,128)}), f32[2,128,16,192]{1,3,0,2:T(8,128)S(1)}, u32[]{:S(2)}, u32[]{:S(2)}) async-start(f32[2,128,16,192]{1,3,0,2:T(8,128)} %pad_maximum_fusion), calls=%async_computation | async-start | bytes 6291456 | tf_op jit(solution)/shard_map/all_to_all | solution.py:185
  64.2 152.6 %all-reduce.30.cloned.1.call-start = ((), (), s32[]{:S(2)}) async-start(), calls=%async_computation.4 | async-start | bytes 524288 | tf_op jit(solution)/shard_map/psum | solution.py:167
  155.0 116.7 %all-gather.5.cloned.1.call-start = ((), (), s32[]{:S(2)}) async-start(), calls=%async_computation.5 | async-start | bytes 4456448 | tf_op jit(solution)/shard_map/all_gather | solution.py:195
  219.2 328.0 %all-gather.7.cloned.1.call-start = ((), (), s32[]{:S(2)}) async-start(), calls=%async_computation.6 | async-start | bytes 8912896 | tf_op jit(solution)/shard_map/all_gather | solution.py:197
  220.2 506.4 %all-gather.9.cloned.1.call-start = ((), (), s32[]{:S(2)}) async-start(), calls=%async_computation.7 | async-start | bytes 4456448 | tf_op jit(solution)/shard_map/all_gather | solution.py:195
  323.0 52.4 %copy-start.51 = (f32[128,128]{1,0:T(8,128)}, f32[128,128]{1,0:T(8,128)S(1)}, u32[]{:S(2)}) copy-start(f32[128,128]{1,0:T(8,128)S(1)} %copy.426) | copy-start | bytes 196612
  324.7 25.6 %copy-start.44 = (f32[128,128]{1,0:T(8,128)}, f32[128,128]{1,0:T(8,128)S(1)}, u32[]{:S(2)}) copy-start(f32[128,128]{1,0:T(8,128)S(1)} %convolution_negate_fusion.13) | copy-start | bytes 196612
  326.1 54.9 %copy-start.3 = (f32[256,256]{0,1:T(8,128)}, f32[256,256]{0,1:T(8,128)S(1)}, u32[]{:S(2)}) copy-start(f32[256,256]{0,1:T(8,128)S(1)} %fusion.133) | copy-start | bytes 786436
  350.6 29.8 %copy-start.45 = (f32[128,128]{1,0:T(8,128)S(1)}, f32[128,128]{1,0:T(8,128)}, u32[]{:S(2)}) copy-start(f32[128,128]{1,0:T(8,128)} %copy-done.44) | copy-start | bytes 196612
  350.9 30.2 %copy-start.16 = (f32[128,128]{0,1:T(8,128)}, f32[128,128]{0,1:T(8,128)S(1)}, u32[]{:S(2)}) copy-start(f32[128,128]{0,1:T(8,128)S(1)} %fusion.170) | copy-start | bytes 196612
  386.0 156.3 %copy-start.1 = (f32[512,512]{0,1:T(8,128)}, f32[512,512]{0,1:T(8,128)S(1)}, u32[]{:S(2)}) copy-start(f32[512,512]{0,1:T(8,128)S(1)} %fusion.51) | copy-start | bytes 3145732
  583.2 11.0 %copy-start.88 = (s32[24]{0:T(128)S(1)}, s32[24]{0:T(128)}, u32[]{:S(2)}) copy-start(s32[24]{0:T(128)} %compare_select_fusion.1) | copy-start | bytes 292
  583.2 11.0 %copy-start.90 = (s32[24]{0:T(128)S(1)}, s32[24]{0:T(128)}, u32[]{:S(2)}) copy-start(s32[24]{0:T(128)} %copy-done.89) | copy-start | bytes 292
  592.9 24.2 %collective-permute-start.1 = (f32[128,2048]{1,0:T(8,128)}, f32[128,2048]{1,0:T(8,128)}, u32[]{:S(2)}, u32[]{:S(2)}) collective-permute-start(f32[128,2048]{1,0:T(8,128)} %convolution_subtract_fusion.1), channel_id=1, source_target_pairs={{0,32},{32,0},{16,48},{48,16},{64,96},{96,64},{80,112},{112,80},{1... | collective-permute-start | bytes 3145736 | tf_op jit(solution)/shard_map/ppermute | solution.py:24
  674.1 12.6 %copy-start.2 = (f32[512,512]{0,1:T(8,128)S(1)}, f32[512,512]{0,1:T(8,128)}, u32[]{:S(2)}) copy-start(f32[512,512]{0,1:T(8,128)} %copy-done.1) | copy-start | bytes 3145732
  674.9 329.0 %all-gather.11.cloned.1.call-start = ((), (), s32[]{:S(2)}) async-start(), calls=%async_computation.8 | async-start | bytes 8912896 | tf_op jit(solution)/shard_map/all_gather | solution.py:197
  679.3 9.7 copy-start.75
  783.3 54.2 %copy-start.50 = (f32[128,128]{1,0:T(8,128)S(1)}, f32[128,128]{1,0:T(8,128)}, u32[]{:S(2)}) copy-start(f32[128,128]{1,0:T(8,128)} %copy-done.49) | copy-start | bytes 196612
  807.1 32.0 %copy-start.20 = (f32[128,256]{1,0:T(8,128)}, f32[128,256]{1,0:T(8,128)S(1)}, u32[]{:S(2)}) copy-start(f32[128,256]{1,0:T(8,128)S(1)} %concatenate.333) | copy-start | bytes 393220
  989.8 11.3 %copy-start.64 = (f32[256,512]{1,0:T(8,128)}, f32[256,512]{1,0:T(8,128)S(1)}, u32[]{:S(2)}) copy-start(f32[256,512]{1,0:T(8,128)S(1)} %concatenate.353) | copy-start | bytes 1572868
  1034.7 9.8 copy-start.15
  (76 other events, 251.2 us)
Sparse Core Ops, SparseCore 0:
  41.0 113.8 reduce-scatter.1
  157.3 59.4 all-reduce.29
  219.5 52.1 all-gather.4
  274.3 70.5 all-gather.6
  675.0 51.4 all-gather.8
  728.5 70.5 all-gather.10

commit v2 on v1

--- a/solution.py
+++ b/solution.py
@@ -3,6 +3,8 @@
 import jax
 import jax.numpy as jnp
 from jax import lax
+from jax.experimental import pallas as pl
+from jax.experimental.pallas import tpu as pltpu
 from jax.sharding import PartitionSpec as P
 
 S = 1024
@@ -12,6 +14,56 @@
 
 
 HIGHEST = lax.Precision.HIGHEST
+HIGH = lax.Precision.HIGH
+SUB = 8
+
+def _outer_t(left, right):
+    return lax.dot_general(left, right, (((0,), (0,)), ((), ())), precision=HIGHEST, preferred_element_type=jnp.float32)
+
+def _kernel(a_ref, l_ref, x_ref, w_ref, t_ref):
+    n = a_ref.shape[0]
+    row = lax.broadcasted_iota(jnp.int32, (n, n), 0)
+    col = lax.broadcasted_iota(jnp.int32, (n, n), 1)
+    a = a_ref[...]
+    w_ref[...] = jnp.where(row >= col, a, a.T)
+    x_ref[...] = jnp.where(row == col, 1.0, 0.0).astype(jnp.float32)
+    sub = lax.broadcasted_iota(jnp.int32, (SUB, n), 0)
+    lane = lax.broadcasted_iota(jnp.int32, (SUB, n), 1)
+    lane1 = lax.broadcasted_iota(jnp.int32, (1, n), 1)
+    sub1 = lax.broadcasted_iota(jnp.int32, (SUB, 1), 0)
+
+    for jb in range(n // SUB):
+        r0 = jb * SUB
+        rows = w_ref[pl.ds(r0, SUB), :]
+        xb = x_ref[pl.ds(r0, SUB), :]
+        panel = jnp.zeros((SUB, n), jnp.float32)
+        for i in range(SUB):
+            c = r0 + i
+            ri = rows[i : i + 1, :]
+            piv = ri[:, c : c + 1]
+            s = lax.rsqrt(piv)
+            li = jnp.where(lane1 >= c, ri * s, 0.0)
+            rc = rows[:, c : c + 1]
+            lk = jnp.where(sub1 > i, rc * s, 0.0)
+            rows = rows - lk * li
+            panel = jnp.where(sub == i, li, panel)
+            xi = xb[i : i + 1, :] * s
+            xb = jnp.where(sub == i, xi, xb - lk * xi)
+        t_ref[pl.ds(r0, SUB), :] = panel
+        x_ref[pl.ds(r0, SUB), :] = xb
+        w_ref[...] = w_ref[...] - _outer_t(panel, panel)
+        below = row >= r0 + SUB
+        x_now = x_ref[...]
+        x_ref[...] = jnp.where(below, x_now - _outer_t(panel, xb), x_now)
+    l_ref[...] = t_ref[...].T
+
+def base_cholesky_inverse(a):
+    n = a.shape[0]
+    return pl.pallas_call(
+        _kernel,
+        out_shape=(jax.ShapeDtypeStruct((n, n), jnp.float32), jax.ShapeDtypeStruct((n, n), jnp.float32)),
+        scratch_shapes=[pltpu.VMEM((n, n), jnp.float32), pltpu.VMEM((n, n), jnp.float32)],
+    )(a)
 
 
 def partner_2(block, axis, bit):
@@ -93,9 +145,7 @@
 def cholesky_inverse(matrix, base_size):
     order = matrix.shape[0]
     if order <= base_size:
-        lower = jnp.linalg.cholesky(matrix)
-        identity = jnp.eye(order, dtype=jnp.float32)
-        return (lower, jax.scipy.linalg.solve_triangular(lower, identity, lower=True))
+        return base_cholesky_inverse(matrix)
     half = order // 2
     lower_11, inverse_11 = cholesky_inverse(matrix[:half, :half], base_size)
     lower_21 = jnp.dot(matrix[half:, :half], inverse_11.T, precision=HIGHEST, preferred_element_type=jnp.float32)
@@ -164,7 +214,9 @@
         0, row_count // step_rows, add_rows, jnp.zeros((target_total, BLK, BLK), jnp.float32)
     )
     per_front = gram_blocks.reshape(front_total, S, BLK)
-    obs_share = lax.psum(lax.psum_scatter(per_front, "inner", scatter_dimension=1, tiled=True), "outer")
+    obs_share = lax.psum_scatter(per_front, "inner", scatter_dimension=1, tiled=True)
+    for bit in range(group_count.bit_length() - 1):
+        obs_share = obs_share + partner_2(obs_share, "outer", bit)
     current = child_update[0]
     pivot_list = []
     border_list = []
@@ -197,14 +249,14 @@
         coupling_all = lax.all_gather(border_front[:, :S], "inner", axis=0, tiled=True)
         pivot_lower, pivot_inverse = cholesky_inverse(pivot_all, BLK)
         border_all = jnp.dot(
-            coupling_all, pivot_inverse.T, precision=HIGHEST, preferred_element_type=jnp.float32
+            coupling_all, pivot_inverse.T, precision=HIGH, preferred_element_type=jnp.float32
         )
         border_factor = lax.dynamic_slice_in_dim(border_all, member * (B // inner_count), B // inner_count, 0)
         product = jnp.einsum(
             "rs,cs->rc",
             border_factor,
             border_all,
-            precision=HIGHEST,
+            precision=HIGH,
             preferred_element_type=jnp.float32,
         )
         current = border_front[:, S:] - product

time: 1060 us -> 802 us (0.76)
  other arithmetic: 460 us -> 47.3 us
  Pallas kernels: 0 us -> 259 us
  blocking collectives: 42.2 us -> 0 us
  matrix products: 169 us -> 141 us
  local copies, waits for them, and re-layouts: 113 us -> 85.2 us
  waiting for transfers between devices: 241 us -> 221 us
  starting transfers between devices: 10.3 us -> 22.2 us
    another operation x80 -> x0, other arithmetic: 406 us -> none  [the longest x48 214 us: cholesky_inverse(): lower = jnp.linalg.cholesky(matrix)]
    pallas_call x0 -> x16, Pallas kernels: none -> 259 us  [base_cholesky_inverse(): pl.pallas_call(_kernel, out_shape=(jax.ShapeDtypeStruct((n, n), jnp.float...]
    psum x1 -> x0, waiting for transfers between devices: 58.8 us -> none  [shards(): lax.psum(lax.psum_scatter(per_front, 'inner', scatter_dimension=1, tiled=...]
    reduce_scatter x1, waiting for transfers between devices: 39.4 us -> 83.1 us  [shards(): lax.psum_scatter(per_front, 'inner', scatter_dimension=1, tiled=True)]
    all_to_all x1 -> x0, blocking collectives: 42.2 us -> none  [shards(): lax.all_to_all(outgoing, 'inner', split_axis=2, concat_axis=1, tiled=True)]
    dot_general x4, matrix products: 86.2 us -> 50.5 us  [the longest x2 39.6 us: shards(): jnp.dot(coupling_all, pivot_inverse.T, precision=HIGH, preferred_element_...]
    another operation x16 -> x0, matrix products: 12.9 us -> none  [cholesky_inverse(): jax.scipy.linalg.solve_triangular(lower, identity, lower=True)]
    div x14 -> x0, other arithmetic: 11.4 us -> none  [cholesky_inverse(): lower = jnp.linalg.cholesky(matrix)]
  transfers between devices with their start and end apart: 9 -> 12, of which waited for: 6 -> 8; matrix products, arithmetic and copies ran while one was open for 59% -> 21% of each run, Pallas kernels for 0% -> 33%
where the time goes in v2:
time: 802 us; the launch traced here: 792 us
  Pallas kernels  259 us (32%)
  waiting for transfers between devices  221 us (28%)
  matrix products  141 us (18%)
  local copies, waits for them, and re-layouts  85.2 us (11%)
  other arithmetic  47.3 us (6%)
  starting transfers between devices  22.2 us (3%)
  between operations  15.8 us (2%)
    pallas_call x16, Pallas kernels, base_cholesky_inverse(): pl.pallas_call(_kernel, out_shape=(jax.ShapeDtypeStruct((n, n), jnp.float...  259 us
    reduce_scatter x1, waiting for transfers between devices, shards(): lax.psum_scatter(per_front, 'inner', scatter_dimension=1, tiled=True)  83.1 us
    all_gather x2, waiting for transfers between devices, shards(): pivot_all = lax.all_gather(sep_front[:, :S], 'inner', axis=0, tiled=True)  81.7 us
    dot_general x2, matrix products, shards(): jnp.dot(coupling_all, pivot_inverse.T, precision=HIGH, preferred_element_...  39.6 us
    all_to_all x2, waiting for transfers between devices, shards(): lax.all_to_all(outgoing, 'inner', split_axis=2, concat_axis=1, tiled=True)  37.5 us
    dot_general x14, matrix products, cholesky_inverse(): jnp.dot(lower_21, lower_21.T, precision=HIGHEST, preferred_element_type=j...  26.1 us
    dot_general x14, matrix products, cholesky_inverse(): jnp.dot(matrix[half:, :half], inverse_11.T, precision=HIGHEST, preferred_...  21.9 us
    ppermute x5, waiting for transfers between devices, partner_2(): return lax.ppermute(block, axis, route)  18.7 us
  transfers between devices with their start and end apart: 12, of which 8 were waited for; matrix products, arithmetic and copies ran while one was open for 21% of the time, Pallas kernels for 33%

profile of v2, /device:TPU:1, one launch (start us, length us, event | category | flops | bytes accessed | tf_op | source)
XLA Modules:
  0.0 791.9 jit_solution(8760582578538428609)
XLA Ops:
  7.2 25.9 %while.14 = (s32[]{:T(128)}, f32[48,128,128]{2,1,0:T(8,128)S(1)}, s32[2048]{0:T(1024)}, bf16[2048,128]{1,0:T(8,128)(2,1)}, s32[]{:T(128)}, /*index=5*/s32[]{:T(128)}, s32[]{:T(128)}, s32[]{:T(128)}) while((s32[]{:T(128)}, f32[48,128,128]{2,1,0:T(8,128)S(1)}, s32[2048]{0:T(1024)}, bf16[2048,128]{1,0:T(8,128)(2,1)}, s32[]{:T(128)}, ...), condition=%wide.region_5.8_spmd.clone, body=%wide.region_4.7_spmd.clone.sunk | while | flops 405823488 | bytes 6737053 | solution.py:213
  63.0 83.1 %reduce-scatter.2.cloned.1.call-done = f32[6,64,128]{2,1,0:T(8,128)} async-done(((f32[6,1024,128]{2,1,0:T(8,128)}), f32[6,64,128]{2,1,0:T(8,128)}) %reduce-scatter.2.cloned.1.call-update) | async-done | bytes 196624 | tf_op jit(solution)/shard_map/reduce_scatter | solution.py:217
  167.4 49.8 %all-gather.5.cloned.1.call-done = f32[1024,1024]{1,0:T(8,128)} async-done(((f32[64,1024]{1,0:T(8,128)}), f32[1024,1024]{1,0:T(8,128)}) %all-gather.5.cloned.1.call-update) | async-done | bytes 4194320 | tf_op jit(solution)/shard_map/all_gather | solution.py:247
  218.7 16.2 %shard_map.67 = (f32[128,128]{1,0:T(8,128)}, f32[128,128]{1,0:T(8,128)}) custom-call(f32[128,128]{1,0:T(8,128)} %slice.290.a_ref), custom_call_target="tpu_custom_call" | custom-call | tf_op jit(solution)/shard_map/pallas_call | solution.py:62
  237.8 16.2 %shard_map.68 = (f32[128,128]{1,0:T(8,128)}, f32[128,128]{1,0:T(8,128)}) custom-call(f32[128,128]{1,0:T(8,128)} %convolution_subtract_fusion.15.a_ref), custom_call_target="tpu_custom_call" | custom-call | tf_op jit(solution)/shard_map/pallas_call | solution.py:62
  259.9 16.3 %shard_map.69 = (f32[128,128]{1,0:T(8,128)}, f32[128,128]{1,0:T(8,128)}) custom-call(f32[128,128]{1,0:T(8,128)} %slice.295.a_ref), custom_call_target="tpu_custom_call" | custom-call | tf_op jit(solution)/shard_map/pallas_call | solution.py:62
  279.1 16.2 %shard_map.70 = (f32[128,128]{1,0:T(8,128)}, f32[128,128]{1,0:T(8,128)}) custom-call(f32[128,128]{1,0:T(8,128)} %convolution_subtract_fusion.14.a_ref), custom_call_target="tpu_custom_call" | custom-call | tf_op jit(solution)/shard_map/pallas_call | solution.py:62
  309.4 16.2 %shard_map.71 = (f32[128,128]{1,0:T(8,128)}, f32[128,128]{1,0:T(8,128)}) custom-call(f32[128,128]{1,0:T(8,128)} %slice.300.a_ref), custom_call_target="tpu_custom_call" | custom-call | tf_op jit(solution)/shard_map/pallas_call | solution.py:62
  329.1 16.2 %shard_map.72 = (f32[128,128]{1,0:T(8,128)}, f32[128,128]{1,0:T(8,128)}) custom-call(f32[128,128]{1,0:T(8,128)} %convolution_subtract_fusion.13.a_ref), custom_call_target="tpu_custom_call" | custom-call | tf_op jit(solution)/shard_map/pallas_call | solution.py:62
  352.5 16.6 %shard_map.73 = (f32[128,128]{1,0:T(8,128)}, f32[128,128]{1,0:T(8,128)}) custom-call(f32[128,128]{1,0:T(8,128)} %slice.305.a_ref), custom_call_target="tpu_custom_call" | custom-call | tf_op jit(solution)/shard_map/pallas_call | solution.py:62
  374.1 16.2 %shard_map.74 = (f32[128,128]{1,0:T(8,128)}, f32[128,128]{1,0:T(8,128)}) custom-call(f32[128,128]{1,0:T(8,128)} %convolution_subtract_fusion.12.a_ref), custom_call_target="tpu_custom_call" | custom-call | tf_op jit(solution)/shard_map/pallas_call | solution.py:62
  401.3 23.1 %fusion.12 = f32[2048,1024]{1,0:T(8,128)S(1)} fusion(f32[2048,1024]{1,0:T(8,128)} %all-gather.7.cloned.1.call-done, f32[512,512]{1,0:T(8,128)S(1)} %copy-done.36, f32[128,128]{1,0:T(8,128)} %get-tuple-element.147, f32[128,128]{1,0:T(8,128)} %copy-done.69, f32[128,256]{1,0:T(8,128)} %concatenate.310, f32[256,256]{1,0:T(8,128)} %copy-done.65, ...), kind=kOutput, calls=%fused_computation.29 | convolution fusion | flops 12893290496 | bytes 19922944 | tf_op jit(solution)/shard_map/dot_general | solution.py:251
  437.9 16.2 %collective-permute-done.4 = f32[128,2048]{1,0:T(8,128)} collective-permute-done((f32[128,2048]{1,0:T(8,128)}, f32[128,2048]{1,0:T(8,128)}, u32[]{:S(2)}, u32[]{:S(2)}) %collective-permute-start.4) | collective-permute-done | bytes 1048608 | tf_op jit(solution)/shard_map/ppermute | solution.py:76
  467.7 37.5 %all-to-all-done.1 = f32[2,128,16,192]{1,3,0,2:T(8,128)S(1)} async-done(((f32[2,128,16,192]{1,3,0,2:T(8,128)}), f32[2,128,16,192]{1,3,0,2:T(8,128)S(1)}, u32[]{:S(2)}, u32[]{:S(2)}) %all-to-all-start.1) | async-done | bytes 3145760 | tf_op jit(solution)/shard_map/all_to_all | solution.py:237
  537.5 31.8 %all-gather.9.cloned.1.call-done = f32[1024,1024]{1,0:T(8,128)} async-done(((f32[64,1024]{1,0:T(8,128)}), f32[1024,1024]{1,0:T(8,128)}) %all-gather.9.cloned.1.call-update) | async-done | bytes 4194320 | tf_op jit(solution)/shard_map/all_gather | solution.py:247
  570.8 16.2 %shard_map.75 = (f32[128,128]{1,0:T(8,128)}, f32[128,128]{1,0:T(8,128)}) custom-call(f32[128,128]{1,0:T(8,128)} %slice.318.a_ref), custom_call_target="tpu_custom_call" | custom-call | tf_op jit(solution)/shard_map/pallas_call | solution.py:62
  590.7 16.2 %shard_map.76 = (f32[128,128]{1,0:T(8,128)}, f32[128,128]{1,0:T(8,128)}) custom-call(f32[128,128]{1,0:T(8,128)} %convolution_subtract_fusion.11.a_ref), custom_call_target="tpu_custom_call" | custom-call | tf_op jit(solution)/shard_map/pallas_call | solution.py:62
  613.6 16.2 %shard_map.77 = (f32[128,128]{1,0:T(8,128)}, f32[128,128]{1,0:T(8,128)}) custom-call(f32[128,128]{1,0:T(8,128)} %slice.323.a_ref), custom_call_target="tpu_custom_call" | custom-call | tf_op jit(solution)/shard_map/pallas_call | solution.py:62
  633.4 16.2 %shard_map.78 = (f32[128,128]{1,0:T(8,128)}, f32[128,128]{1,0:T(8,128)}) custom-call(f32[128,128]{1,0:T(8,128)} %convolution_subtract_fusion.10.a_ref), custom_call_target="tpu_custom_call" | custom-call | tf_op jit(solution)/shard_map/pallas_call | solution.py:62
  663.8 16.2 %shard_map.79 = (f32[128,128]{1,0:T(8,128)}, f32[128,128]{1,0:T(8,128)}) custom-call(f32[128,128]{1,0:T(8,128)} %slice.328.a_ref), custom_call_target="tpu_custom_call" | custom-call | tf_op jit(solution)/shard_map/pallas_call | solution.py:62
  683.6 16.2 %shard_map.80 = (f32[128,128]{1,0:T(8,128)}, f32[128,128]{1,0:T(8,128)}) custom-call(f32[128,128]{1,0:T(8,128)} %convolution_subtract_fusion.9.a_ref), custom_call_target="tpu_custom_call" | custom-call | tf_op jit(solution)/shard_map/pallas_call | solution.py:62
  709.4 16.2 %shard_map.81 = (f32[128,128]{1,0:T(8,128)}, f32[128,128]{1,0:T(8,128)}) custom-call(f32[128,128]{1,0:T(8,128)} %slice.333.a_ref), custom_call_target="tpu_custom_call" | custom-call | tf_op jit(solution)/shard_map/pallas_call | solution.py:62
  730.6 16.2 %shard_map.82 = (f32[128,128]{1,0:T(8,128)}, f32[128,128]{1,0:T(8,128)}) custom-call(f32[128,128]{1,0:T(8,128)} %convolution_subtract_fusion.8.a_ref), custom_call_target="tpu_custom_call" | custom-call | tf_op jit(solution)/shard_map/pallas_call | solution.py:62
  762.0 16.5 %fusion.10 = f32[2048,1024]{1,0:T(8,128)S(1)} fusion(f32[2048,1024]{1,0:T(8,128)} %all-gather.11.cloned.1.call-done, f32[512,512]{1,0:T(8,128)S(1)} %copy-done.35, f32[128,128]{1,0:T(8,128)} %get-tuple-element.163, f32[128,128]{1,0:T(8,128)} %copy-done.68, f32[128,256]{1,0:T(8,128)S(1)} %copy-done.59, f32[256,256]{1,0:T(8,128)} %copy-done.64, ...), kind=kOutput, calls=%fused_computation.23 | convolution fusion | flops 12893290496 | bytes 19922944 | tf_op jit(solution)/shard_map/dot_general | solution.py:251
  (418 shorter events, 258.3 us)
Async XLA Ops:
  7.2 138.9 %reduce-scatter.2.cloned.1.call-start = ((), (), s32[]{:S(2)}) async-start(), calls=%async_computation.3 | async-start | bytes 3342336 | tf_op jit(solution)/shard_map/reduce_scatter | solution.py:217
  37.4 9.8 %collective-permute-start = (f32[128,2048]{0,1:T(8,128)}, f32[128,2048]{0,1:T(8,128)}, u32[]{:S(2)}, u32[]{:S(2)}) collective-permute-start(f32[128,2048]{0,1:T(8,128)} %bitcast.8), channel_id=1, source_target_pairs={{0,16},{16,0},{32,48},{48,32},{64,80},{80,64},{96,112},{112,96},{1... | collective-permute-start | bytes 3145736 | tf_op jit(solution)/shard_map/ppermute | solution.py:76
  56.0 92.4 %all-to-all-start = ((f32[2,128,16,192]{1,3,0,2:T(8,128)}), f32[2,128,16,192]{1,3,0,2:T(8,128)S(1)}, u32[]{:S(2)}, u32[]{:S(2)}) async-start(f32[2,128,16,192]{1,3,0,2:T(8,128)} %pad_maximum_fusion), calls=%async_computation | async-start | bytes 6291456 | tf_op jit(solution)/shard_map/all_to_all | solution.py:237
  62.9 154.3 %all-gather.5.cloned.1.call-start = ((), (), s32[]{:S(2)}) async-start(), calls=%async_computation.4 | async-start | bytes 4456448 | tf_op jit(solution)/shard_map/all_gather | solution.py:247
  146.1 3.7 collective-permute-start.1
  150.8 6.2 collective-permute-start.2
  156.9 6.8 collective-permute-start.3
  165.2 236.1 %all-gather.7.cloned.1.call-start = ((), (), s32[]{:S(2)}) async-start(), calls=%async_computation.5 | async-start | bytes 8912896 | tf_op jit(solution)/shard_map/all_gather | solution.py:249
  234.9 60.4 %copy-start.21 = (f32[128,128]{1,0:T(8,128)S(1)}, f32[128,128]{1,0:T(8,128)}, u32[]{:S(2)}) copy-start(f32[128,128]{1,0:T(8,128)} %get-tuple-element.133) | copy-start | bytes 196612
  254.0 44.5 %copy-start.44 = (f32[128,128]{1,0:T(8,128)S(1)}, f32[128,128]{1,0:T(8,128)}, u32[]{:S(2)}) copy-start(f32[128,128]{1,0:T(8,128)} %get-tuple-element.135) | copy-start | bytes 196612
  257.6 41.5 %copy-start.4 = (f32[256,256]{0,1:T(8,128)}, f32[256,256]{0,1:T(8,128)S(1)}, u32[]{:S(2)}) copy-start(f32[256,256]{0,1:T(8,128)S(1)} %fusion.101) | copy-start | bytes 786436
  277.0 22.0 %copy-start.24 = (f32[128,256]{1,0:T(8,128)}, f32[128,256]{1,0:T(8,128)S(1)}, u32[]{:S(2)}) copy-start(f32[128,256]{1,0:T(8,128)S(1)} %concatenate.289) | copy-start | bytes 393220
  304.1 92.2 %copy-start.2 = (f32[512,512]{0,1:T(8,128)}, f32[512,512]{0,1:T(8,128)S(1)}, u32[]{:S(2)}) copy-start(f32[512,512]{0,1:T(8,128)S(1)} %fusion.51) | copy-start | bytes 3145732
  429.9 24.2 %collective-permute-start.4 = (f32[128,2048]{1,0:T(8,128)}, f32[128,2048]{1,0:T(8,128)}, u32[]{:S(2)}, u32[]{:S(2)}) collective-permute-start(f32[128,2048]{1,0:T(8,128)} %convolution_subtract_fusion.1), channel_id=1, source_target_pairs={{0,32},{32,0},{16,48},{48,16},{64,96},{96,64},{80,112},{112,80},{1... | collective-permute-start | bytes 3145736 | tf_op jit(solution)/shard_map/ppermute | solution.py:76
  462.7 42.5 %all-to-all-start.1 = ((f32[2,128,16,192]{1,3,0,2:T(8,128)}), f32[2,128,16,192]{1,3,0,2:T(8,128)S(1)}, u32[]{:S(2)}, u32[]{:S(2)}) async-start(f32[2,128,16,192]{1,3,0,2:T(8,128)} %pad_maximum_fusion.1), calls=%async_computation.2 | async-start | bytes 6291456 | tf_op jit(solution)/shard_map/all_to_all | solution.py:237
  467.6 101.7 %all-gather.9.cloned.1.call-start = ((), (), s32[]{:S(2)}) async-start(), calls=%async_computation.6 | async-start | bytes 4456448 | tf_op jit(solution)/shard_map/all_gather | solution.py:247
  514.3 12.0 %copy-start.3 = (f32[512,512]{0,1:T(8,128)S(1)}, f32[512,512]{0,1:T(8,128)}, u32[]{:S(2)}) copy-start(f32[512,512]{0,1:T(8,128)} %copy-done.2) | copy-start | bytes 3145732
  514.3 247.8 %all-gather.11.cloned.1.call-start = ((), (), s32[]{:S(2)}) async-start(), calls=%async_computation.7 | async-start | bytes 8912896 | tf_op jit(solution)/shard_map/all_gather | solution.py:249
  587.0 62.6 %copy-start.19 = (f32[128,128]{1,0:T(8,128)S(1)}, f32[128,128]{1,0:T(8,128)}, u32[]{:S(2)}) copy-start(f32[128,128]{1,0:T(8,128)} %get-tuple-element.149) | copy-start | bytes 196612
  606.8 42.8 %copy-start.43 = (f32[128,128]{1,0:T(8,128)S(1)}, f32[128,128]{1,0:T(8,128)}, u32[]{:S(2)}) copy-start(f32[128,128]{1,0:T(8,128)} %get-tuple-element.151) | copy-start | bytes 196612
  630.6 27.1 %copy-start.22 = (f32[128,256]{1,0:T(8,128)}, f32[128,256]{1,0:T(8,128)S(1)}, u32[]{:S(2)}) copy-start(f32[128,256]{1,0:T(8,128)S(1)} %concatenate.333) | copy-start | bytes 393220
  680.0 66.9 %copy-start.18 = (f32[128,128]{1,0:T(8,128)S(1)}, f32[128,128]{1,0:T(8,128)}, u32[]{:S(2)}) copy-start(f32[128,128]{1,0:T(8,128)} %get-tuple-element.157) | copy-start | bytes 196612
  702.0 23.6 %copy-start.40 = (f32[128,128]{1,0:T(8,128)}, f32[128,128]{1,0:T(8,128)S(1)}, u32[]{:S(2)}) copy-start(f32[128,128]{1,0:T(8,128)S(1)} %convolution_negate_fusion.7) | copy-start | bytes 196612
  747.8 11.4 %copy-start.56 = (f32[256,512]{1,0:T(8,128)}, f32[256,512]{1,0:T(8,128)S(1)}, u32[]{:S(2)}) copy-start(f32[256,512]{1,0:T(8,128)S(1)} %concatenate.353) | copy-start | bytes 1572868
  (75 other events, 253.0 us)
Sparse Core Ops, SparseCore 0:
  35.0 111.0 reduce-scatter.1
  165.3 51.8 all-gather.4
  219.9 70.7 all-gather.6
  514.4 54.9 all-gather.8
  571.4 70.5 all-gather.10

commit v3 on v2

--- a/solution.py
+++ b/solution.py
@@ -148,13 +148,13 @@
         return base_cholesky_inverse(matrix)
     half = order // 2
     lower_11, inverse_11 = cholesky_inverse(matrix[:half, :half], base_size)
-    lower_21 = jnp.dot(matrix[half:, :half], inverse_11.T, precision=HIGHEST, preferred_element_type=jnp.float32)
-    schur = matrix[half:, half:] - jnp.dot(lower_21, lower_21.T, precision=HIGHEST, preferred_element_type=jnp.float32)
+    lower_21 = jnp.dot(matrix[half:, :half], inverse_11.T, precision=HIGH, preferred_element_type=jnp.float32)
+    schur = matrix[half:, half:] - jnp.dot(lower_21, lower_21.T, precision=HIGH, preferred_element_type=jnp.float32)
     lower_22, inverse_22 = cholesky_inverse(schur, base_size)
     inverse_21 = -jnp.dot(
         inverse_22,
-        jnp.dot(lower_21, inverse_11, precision=HIGHEST, preferred_element_type=jnp.float32),
-        precision=HIGHEST,
+        jnp.dot(lower_21, inverse_11, precision=HIGH, preferred_element_type=jnp.float32),
+        precision=HIGH,
         preferred_element_type=jnp.float32,
     )
     zero = jnp.zeros((half, half), jnp.float32)
@@ -214,9 +214,28 @@
         0, row_count // step_rows, add_rows, jnp.zeros((target_total, BLK, BLK), jnp.float32)
     )
     per_front = gram_blocks.reshape(front_total, S, BLK)
-    obs_share = lax.psum_scatter(per_front, "inner", scatter_dimension=1, tiled=True)
-    for bit in range(group_count.bit_length() - 1):
-        obs_share = obs_share + partner_2(obs_share, "outer", bit)
+    half = group_index >> 2 & 1
+    pair = group_index >> 1 & 1
+    kept = jnp.concatenate(
+        [
+            lax.dynamic_slice_in_dim(per_front, 2 * half, 2, 0),
+            lax.dynamic_slice_in_dim(per_front, 4 + half, 1, 0),
+        ]
+    )
+    given = jnp.concatenate(
+        [
+            lax.dynamic_slice_in_dim(per_front, 2 - 2 * half, 2, 0),
+            lax.dynamic_slice_in_dim(per_front, 5 - half, 1, 0),
+        ]
+    )
+    kept = kept + partner_2(given, "outer", 2)
+    given = jnp.stack([lax.dynamic_index_in_dim(kept, 1 - pair, 0, keepdims=False), kept[2]])
+    arrived = partner_2(given, "outer", 1)
+    kept = jnp.stack(
+        [lax.dynamic_index_in_dim(kept, pair, 0, keepdims=False) + arrived[0], kept[2] + arrived[1]]
+    )
+    kept = kept + partner_2(kept, "outer", 0)
+    obs_share = lax.psum_scatter(kept, "inner", scatter_dimension=1, tiled=True)
     current = child_update[0]
     pivot_list = []
     border_list = []
@@ -239,7 +258,7 @@
         sib_cols = parent_rows(arrived[1, :, 0, :], sib_map, parent_count)
         front_rows = (own_cols + sib_cols).T
         front_slot = front_offset + (group_index >> level_index + 1)
-        obs_rows = lax.dynamic_index_in_dim(obs_share, front_slot, 0, keepdims=False)
+        obs_rows = obs_share[level_index]
         sep_front = front_rows[:sep_rows]
         block_now = lax.dynamic_slice_in_dim(sep_front, block_start, BLK, 1)
         sep_front = lax.dynamic_update_slice_in_dim(sep_front, block_now + obs_rows, block_start, 1)

time: 802 us -> 822 us (1.025)
  blocking collectives: 0 us -> 42.2 us
  matrix products: 141 us -> 130 us
  waiting for transfers between devices: 221 us -> 210 us
    all_to_all x0 -> x1, blocking collectives: none -> 42.2 us  [shards(): lax.all_to_all(outgoing, 'inner', split_axis=2, concat_axis=1, tiled=True)]
    ppermute x5, waiting for transfers between devices: 18.7 us -> 54.6 us  [partner_2(): return lax.ppermute(block, axis, route)]
    reduce_scatter x1, waiting for transfers between devices: 83.1 us -> 50.1 us  [shards(): obs_share = lax.psum_scatter(kept, 'inner', scatter_dimension=1, tiled=True)]
    all_to_all x2 -> x1, waiting for transfers between devices: 37.5 us -> 25.6 us  [shards(): lax.all_to_all(outgoing, 'inner', split_axis=2, concat_axis=1, tiled=True)]
    dot_general x56, matrix products: 78.4 us -> 66.8 us  [the longest x14 22.5 us: cholesky_inverse(): jnp.dot(lower_21, lower_21.T, precision=HIGH, preferred_element_type=jnp....]
  transfers between devices with their start and end apart: 12 -> 11, of which waited for: 8 -> 8; matrix products, arithmetic and copies ran while one was open for 21% -> 23% of each run, Pallas kernels for 33% -> 32%
where the time goes in v3:
time: 822 us; the launch traced here: 811 us
  Pallas kernels  260 us (32%)
  waiting for transfers between devices  210 us (26%)
  matrix products  130 us (16%)
  local copies, waits for them, and re-layouts  85.8 us (10%)
  other arithmetic  50.7 us (6%)
  blocking collectives  42.2 us (5%)
  starting transfers between devices  16.3 us (2%)
  between operations  15.7 us (2%)
    pallas_call x16, Pallas kernels, base_cholesky_inverse(): pl.pallas_call(_kernel, out_shape=(jax.ShapeDtypeStruct((n, n), jnp.float...  260 us
    all_gather x2, waiting for transfers between devices, shards(): pivot_all = lax.all_gather(sep_front[:, :S], 'inner', axis=0, tiled=True)  79.5 us
    ppermute x5, waiting for transfers between devices, partner_2(): return lax.ppermute(block, axis, route)  54.6 us
    reduce_scatter x1, waiting for transfers between devices, shards(): obs_share = lax.psum_scatter(kept, 'inner', scatter_dimension=1, tiled=True)  50.1 us
    all_to_all x1, blocking collectives, shards(): lax.all_to_all(outgoing, 'inner', split_axis=2, concat_axis=1, tiled=True)  42.2 us
    dot_general x2, matrix products, shards(): jnp.dot(coupling_all, pivot_inverse.T, precision=HIGH, preferred_element_...  40.2 us
    all_to_all x1, waiting for transfers between devices, shards(): lax.all_to_all(outgoing, 'inner', split_axis=2, concat_axis=1, tiled=True)  25.6 us
    dot_general x14, matrix products, cholesky_inverse(): jnp.dot(lower_21, lower_21.T, precision=HIGH, preferred_element_type=jnp....  22.5 us
  transfers between devices with their start and end apart: 11, of which 8 were waited for; matrix products, arithmetic and copies ran while one was open for 23% of the time, Pallas kernels for 32%

profile of v3, /device:TPU:1, one launch (start us, length us, event | category | flops | bytes accessed | tf_op | source)
XLA Modules:
  0.0 811.0 jit_solution(5533982266820986323)
XLA Ops:
  11.1 25.9 %while.14 = (s32[]{:T(128)}, f32[48,128,128]{2,1,0:T(8,128)S(1)}, s32[2048]{0:T(1024)}, bf16[2048,128]{1,0:T(8,128)(2,1)}, s32[]{:T(128)}, /*index=5*/s32[]{:T(128)}, s32[]{:T(128)}, s32[]{:T(128)}) while((s32[]{:T(128)}, f32[48,128,128]{2,1,0:T(8,128)S(1)}, s32[2048]{0:T(1024)}, bf16[2048,128]{1,0:T(8,128)(2,1)}, s32[]{:T(128)}, ...), condition=%wide.region_5.8_spmd.clone, body=%wide.region_4.7_spmd.clone.sunk | while | flops 405823488 | bytes 6737053 | solution.py:213
  51.2 27.9 %collective-permute-done.1 = f32[3,1024,128]{2,1,0:T(8,128)} collective-permute-done((f32[3,1024,128]{2,1,0:T(8,128)}, f32[3,1024,128]{2,1,0:T(8,128)}, u32[]{:S(2)}, u32[]{:S(2)}) %collective-permute-start.1) | collective-permute-done | bytes 1572896 | tf_op jit(solution)/shard_map/ppermute | solution.py:76
  114.1 25.6 %all-to-all-done = f32[2,128,16,192]{1,3,0,2:T(8,128)S(1)} async-done(((f32[2,128,16,192]{1,3,0,2:T(8,128)}), f32[2,128,16,192]{1,3,0,2:T(8,128)S(1)}, u32[]{:S(2)}, u32[]{:S(2)}) %all-to-all-start) | async-done | bytes 3145760 | tf_op jit(solution)/shard_map/all_to_all | solution.py:256
  147.2 50.1 %reduce-scatter.2.cloned.1.call-done = f32[2,64,128]{2,1,0:T(8,128)} async-done(((f32[2,1024,128]{2,1,0:T(8,128)}), f32[2,64,128]{2,1,0:T(8,128)}) %reduce-scatter.2.cloned.1.call-update) | async-done | bytes 65552 | tf_op jit(solution)/shard_map/reduce_scatter | solution.py:238
  201.0 51.2 %all-gather.5.cloned.1.call-done = f32[1024,1024]{1,0:T(8,128)} async-done(((f32[64,1024]{1,0:T(8,128)}), f32[1024,1024]{1,0:T(8,128)}) %all-gather.5.cloned.1.call-update) | async-done | bytes 4194320 | tf_op jit(solution)/shard_map/all_gather | solution.py:266
  253.8 16.2 %shard_map.67 = (f32[128,128]{1,0:T(8,128)}, f32[128,128]{1,0:T(8,128)}) custom-call(f32[128,128]{1,0:T(8,128)} %slice.315.a_ref), custom_call_target="tpu_custom_call" | custom-call | tf_op jit(solution)/shard_map/pallas_call | solution.py:62
  272.8 16.2 %shard_map.68 = (f32[128,128]{1,0:T(8,128)}, f32[128,128]{1,0:T(8,128)}) custom-call(f32[128,128]{1,0:T(8,128)} %convolution_subtract_fusion.15.a_ref), custom_call_target="tpu_custom_call" | custom-call | tf_op jit(solution)/shard_map/pallas_call | solution.py:62
  294.5 16.3 %shard_map.69 = (f32[128,128]{1,0:T(8,128)}, f32[128,128]{1,0:T(8,128)}) custom-call(f32[128,128]{1,0:T(8,128)} %slice.320.a_ref), custom_call_target="tpu_custom_call" | custom-call | tf_op jit(solution)/shard_map/pallas_call | solution.py:62
  313.7 16.2 %shard_map.70 = (f32[128,128]{1,0:T(8,128)}, f32[128,128]{1,0:T(8,128)}) custom-call(f32[128,128]{1,0:T(8,128)} %convolution_subtract_fusion.14.a_ref), custom_call_target="tpu_custom_call" | custom-call | tf_op jit(solution)/shard_map/pallas_call | solution.py:62
  341.8 16.4 %shard_map.71 = (f32[128,128]{1,0:T(8,128)}, f32[128,128]{1,0:T(8,128)}) custom-call(f32[128,128]{1,0:T(8,128)} %slice.325.a_ref), custom_call_target="tpu_custom_call" | custom-call | tf_op jit(solution)/shard_map/pallas_call | solution.py:62
  384.6 16.2 %shard_map.73 = (f32[128,128]{1,0:T(8,128)}, f32[128,128]{1,0:T(8,128)}) custom-call(f32[128,128]{1,0:T(8,128)} %slice.330.a_ref), custom_call_target="tpu_custom_call" | custom-call | tf_op jit(solution)/shard_map/pallas_call | solution.py:62
  405.7 16.6 %shard_map.74 = (f32[128,128]{1,0:T(8,128)}, f32[128,128]{1,0:T(8,128)}) custom-call(f32[128,128]{1,0:T(8,128)} %convolution_subtract_fusion.12.a_ref), custom_call_target="tpu_custom_call" | custom-call | tf_op jit(solution)/shard_map/pallas_call | solution.py:62
  431.2 23.5 %fusion.12 = f32[2048,1024]{1,0:T(8,128)S(1)} fusion(f32[2048,1024]{1,0:T(8,128)} %all-gather.7.cloned.1.call-done, f32[512,512]{1,0:T(8,128)S(1)} %copy-done.38, f32[128,128]{1,0:T(8,128)} %get-tuple-element.147, f32[128,128]{1,0:T(8,128)} %copy-done.70, f32[128,256]{1,0:T(8,128)} %concatenate.318, f32[256,256]{1,0:T(8,128)} %copy-done.66, ...), kind=kOutput, calls=%fused_computation.29 | convolution fusion | flops 12893290496 | bytes 19922944 | tf_op jit(solution)/shard_map/dot_general | solution.py:270
  468.2 16.2 %collective-permute-done.4 = f32[128,2048]{1,0:T(8,128)} collective-permute-done((f32[128,2048]{1,0:T(8,128)}, f32[128,2048]{1,0:T(8,128)}, u32[]{:S(2)}, u32[]{:S(2)}) %collective-permute-start.4) | collective-permute-done | bytes 1048608 | tf_op jit(solution)/shard_map/ppermute | solution.py:76
  491.4 42.2 %all_to_all.30 = f32[2,128,16,192]{1,3,0,2:T(8,128)S(1)} all-to-all(f32[2,128,16,192]{1,3,0,2:T(8,128)S(1)} %pad_maximum_fusion.1), channel_id=1, replica_groups=mesh['outer'=8,'inner'=16] {'inner'}, dimensions={2} | all-to-all | bytes 6291456 | tf_op jit(solution)/shard_map/all_to_all | solution.py:256
  565.4 28.3 %all-gather.9.cloned.1.call-done = f32[1024,1024]{1,0:T(8,128)} async-done(((f32[64,1024]{1,0:T(8,128)}), f32[1024,1024]{1,0:T(8,128)}) %all-gather.9.cloned.1.call-update) | async-done | bytes 4194320 | tf_op jit(solution)/shard_map/all_gather | solution.py:266
  595.1 16.2 %shard_map.75 = (f32[128,128]{1,0:T(8,128)}, f32[128,128]{1,0:T(8,128)}) custom-call(f32[128,128]{1,0:T(8,128)} %slice.344.a_ref), custom_call_target="tpu_custom_call" | custom-call | tf_op jit(solution)/shard_map/pallas_call | solution.py:62
  614.9 16.2 %shard_map.76 = (f32[128,128]{1,0:T(8,128)}, f32[128,128]{1,0:T(8,128)}) custom-call(f32[128,128]{1,0:T(8,128)} %convolution_subtract_fusion.11.a_ref), custom_call_target="tpu_custom_call" | custom-call | tf_op jit(solution)/shard_map/pallas_call | solution.py:62
  637.3 16.4 %shard_map.77 = (f32[128,128]{1,0:T(8,128)}, f32[128,128]{1,0:T(8,128)}) custom-call(f32[128,128]{1,0:T(8,128)} %slice.349.a_ref), custom_call_target="tpu_custom_call" | custom-call | tf_op jit(solution)/shard_map/pallas_call | solution.py:62
  657.2 16.2 %shard_map.78 = (f32[128,128]{1,0:T(8,128)}, f32[128,128]{1,0:T(8,128)}) custom-call(f32[128,128]{1,0:T(8,128)} %convolution_subtract_fusion.10.a_ref), custom_call_target="tpu_custom_call" | custom-call | tf_op jit(solution)/shard_map/pallas_call | solution.py:62
  685.3 16.3 %shard_map.79 = (f32[128,128]{1,0:T(8,128)}, f32[128,128]{1,0:T(8,128)}) custom-call(f32[128,128]{1,0:T(8,128)} %slice.354.a_ref), custom_call_target="tpu_custom_call" | custom-call | tf_op jit(solution)/shard_map/pallas_call | solution.py:62
  730.2 16.6 %shard_map.81 = (f32[128,128]{1,0:T(8,128)}, f32[128,128]{1,0:T(8,128)}) custom-call(f32[128,128]{1,0:T(8,128)} %slice.359.a_ref), custom_call_target="tpu_custom_call" | custom-call | tf_op jit(solution)/shard_map/pallas_call | solution.py:62
  751.8 16.2 %shard_map.82 = (f32[128,128]{1,0:T(8,128)}, f32[128,128]{1,0:T(8,128)}) custom-call(f32[128,128]{1,0:T(8,128)} %convolution_subtract_fusion.8.a_ref), custom_call_target="tpu_custom_call" | custom-call | tf_op jit(solution)/shard_map/pallas_call | solution.py:62
  781.0 16.7 %fusion.10 = f32[2048,1024]{1,0:T(8,128)S(1)} fusion(f32[2048,1024]{1,0:T(8,128)} %all-gather.11.cloned.1.call-done, f32[512,512]{1,0:T(8,128)S(1)} %copy-done.37, f32[128,128]{1,0:T(8,128)} %get-tuple-element.163, f32[128,128]{1,0:T(8,128)} %copy-done.69, f32[128,256]{1,0:T(8,128)S(1)} %copy-done.61, f32[256,256]{1,0:T(8,128)} %copy-done.65, ...), kind=kOutput, calls=%fused_computation.23 | convolution fusion | flops 12893290496 | bytes 19922944 | tf_op jit(solution)/shard_map/dot_general | solution.py:270
  (413 shorter events, 285.3 us)
Async XLA Ops:
  9.7 73.9 %collective-permute-start = (f32[128,2048]{0,1:T(8,128)}, f32[128,2048]{0,1:T(8,128)}, u32[]{:S(2)}, u32[]{:S(2)}) collective-permute-start(f32[128,2048]{0,1:T(8,128)} %bitcast.8), channel_id=1, source_target_pairs={{0,16},{16,0},{32,48},{48,32},{64,80},{80,64},{96,112},{112,96},{1... | collective-permute-start | bytes 3145736 | tf_op jit(solution)/shard_map/ppermute | solution.py:76
  40.2 38.9 %collective-permute-start.1 = (f32[3,1024,128]{2,1,0:T(8,128)}, f32[3,1024,128]{2,1,0:T(8,128)}, u32[]{:S(2)}, u32[]{:S(2)}) collective-permute-start(f32[3,1024,128]{2,1,0:T(8,128)} %pad_maximum_fusion.2), channel_id=1, source_target_pairs={{0,64},{64,0},{16,80},{80,16},{32,96},{96,32},{48,112},{112,48},{1... | collective-permute-start | bytes 4718600 | tf_op jit(solution)/shard_map/ppermute | solution.py:76
  44.1 156.2 %copy-start.80 = (s32[24]{0:T(128)}, s32[24]{0:T(128)S(1)}, u32[]{:S(2)}) copy-start(s32[24]{0:T(128)S(1)} %get-tuple-element.209) | copy-start | bytes 292
  49.7 29.4 %copy-start.10 = (f32[2,1024,128]{2,1,0:T(8,128)S(1)}, f32[2,1024,128]{2,1,0:T(8,128)}, u32[]{:S(2)}) copy-start(f32[2,1024,128]{2,1,0:T(8,128)} %get-tuple-element.193) | copy-start | bytes 3145732
  49.7 29.4 %copy-start.16 = (f32[1,1024,128]{2,1,0:T(8,128)S(1)}, f32[1,1024,128]{2,1,0:T(8,128)}, u32[]{:S(2)}) copy-start(f32[1,1024,128]{2,1,0:T(8,128)} %get-tuple-element.195) | copy-start | bytes 1572868
  82.9 24.5 %collective-permute-start.2 = (f32[2,1024,128]{2,1,0:T(8,128)}, f32[2,1024,128]{2,1,0:T(8,128)}, u32[]{:S(2)}, u32[]{:S(2)}) collective-permute-start(f32[2,1024,128]{2,1,0:T(8,128)} %pad_maximum_fusion.3), channel_id=1, source_target_pairs={{0,32},{32,0},{16,48},{48,16},{64,96},{96,64},{80,112},{112,80},{1... | collective-permute-start | bytes 3145736 | tf_op jit(solution)/shard_map/ppermute | solution.py:76
  92.4 47.3 %all-to-all-start = ((f32[2,128,16,192]{1,3,0,2:T(8,128)}), f32[2,128,16,192]{1,3,0,2:T(8,128)S(1)}, u32[]{:S(2)}, u32[]{:S(2)}) async-start(f32[2,128,16,192]{1,3,0,2:T(8,128)} %pad_maximum_fusion), calls=%async_computation | async-start | bytes 6291456 | tf_op jit(solution)/shard_map/all_to_all | solution.py:256
  99.1 98.2 %reduce-scatter.2.cloned.1.call-start = ((), (), s32[]{:S(2)}) async-start(), calls=%async_computation.3 | async-start | bytes 1114112 | tf_op jit(solution)/shard_map/reduce_scatter | solution.py:238
  109.2 3.7 collective-permute-start.3
  114.0 138.3 %all-gather.5.cloned.1.call-start = ((), (), s32[]{:S(2)}) async-start(), calls=%async_computation.4 | async-start | bytes 4456448 | tf_op jit(solution)/shard_map/all_gather | solution.py:266
  198.8 232.4 %all-gather.7.cloned.1.call-start = ((), (), s32[]{:S(2)}) async-start(), calls=%async_computation.5 | async-start | bytes 8912896 | tf_op jit(solution)/shard_map/all_gather | solution.py:268
  199.7 393.9 %all-gather.9.cloned.1.call-start = ((), (), s32[]{:S(2)}) async-start(), calls=%async_computation.6 | async-start | bytes 4456448 | tf_op jit(solution)/shard_map/all_gather | solution.py:266
  269.9 60.0 %copy-start.23 = (f32[128,128]{1,0:T(8,128)S(1)}, f32[128,128]{1,0:T(8,128)}, u32[]{:S(2)}) copy-start(f32[128,128]{1,0:T(8,128)} %get-tuple-element.133) | copy-start | bytes 196612
  289.0 44.0 %copy-start.46 = (f32[128,128]{1,0:T(8,128)S(1)}, f32[128,128]{1,0:T(8,128)}, u32[]{:S(2)}) copy-start(f32[128,128]{1,0:T(8,128)} %get-tuple-element.135) | copy-start | bytes 196612
  292.5 40.9 %copy-start.4 = (f32[256,256]{0,1:T(8,128)}, f32[256,256]{0,1:T(8,128)S(1)}, u32[]{:S(2)}) copy-start(f32[256,256]{0,1:T(8,128)S(1)} %fusion.101) | copy-start | bytes 786436
  311.7 21.7 %copy-start.26 = (f32[128,256]{1,0:T(8,128)}, f32[128,256]{1,0:T(8,128)S(1)}, u32[]{:S(2)}) copy-start(f32[128,256]{1,0:T(8,128)S(1)} %concatenate.297) | copy-start | bytes 393220
  337.5 90.5 %copy-start.1 = (f32[512,512]{0,1:T(8,128)}, f32[512,512]{0,1:T(8,128)S(1)}, u32[]{:S(2)}) copy-start(f32[512,512]{0,1:T(8,128)S(1)} %fusion.51) | copy-start | bytes 3145732
  460.2 24.2 %collective-permute-start.4 = (f32[128,2048]{1,0:T(8,128)}, f32[128,2048]{1,0:T(8,128)}, u32[]{:S(2)}, u32[]{:S(2)}) collective-permute-start(f32[128,2048]{1,0:T(8,128)} %convolution_subtract_fusion.1), channel_id=1, source_target_pairs={{0,32},{32,0},{16,48},{48,16},{64,96},{96,64},{80,112},{112,80},{1... | collective-permute-start | bytes 3145736 | tf_op jit(solution)/shard_map/ppermute | solution.py:76
  542.1 238.9 %all-gather.11.cloned.1.call-start = ((), (), s32[]{:S(2)}) async-start(), calls=%async_computation.7 | async-start | bytes 8912896 | tf_op jit(solution)/shard_map/all_gather | solution.py:268
  611.3 62.1 %copy-start.21 = (f32[128,128]{1,0:T(8,128)S(1)}, f32[128,128]{1,0:T(8,128)}, u32[]{:S(2)}) copy-start(f32[128,128]{1,0:T(8,128)} %get-tuple-element.149) | copy-start | bytes 196612
  631.1 42.4 %copy-start.45 = (f32[128,128]{1,0:T(8,128)S(1)}, f32[128,128]{1,0:T(8,128)}, u32[]{:S(2)}) copy-start(f32[128,128]{1,0:T(8,128)} %get-tuple-element.151) | copy-start | bytes 196612
  654.5 25.6 %copy-start.24 = (f32[128,256]{1,0:T(8,128)}, f32[128,256]{1,0:T(8,128)S(1)}, u32[]{:S(2)}) copy-start(f32[128,256]{1,0:T(8,128)S(1)} %concatenate.341) | copy-start | bytes 393220
  701.7 66.3 %copy-start.20 = (f32[128,128]{1,0:T(8,128)S(1)}, f32[128,128]{1,0:T(8,128)}, u32[]{:S(2)}) copy-start(f32[128,128]{1,0:T(8,128)} %get-tuple-element.157) | copy-start | bytes 196612
  723.5 23.2 %copy-start.42 = (f32[128,128]{1,0:T(8,128)}, f32[128,128]{1,0:T(8,128)S(1)}, u32[]{:S(2)}) copy-start(f32[128,128]{1,0:T(8,128)S(1)} %convolution_negate_fusion.7) | copy-start | bytes 196612
  (69 other events, 235.7 us)
Sparse Core Ops, SparseCore 0:
  114.1 83.1 reduce-scatter.1
  200.0 52.2 all-gather.4
  255.0 70.4 all-gather.6
  542.2 51.4 all-gather.8
  595.6 70.6 all-gather.10

commit v4 on v1

--- a/solution.py
+++ b/solution.py
@@ -3,6 +3,8 @@
 import jax
 import jax.numpy as jnp
 from jax import lax
+from jax.experimental import pallas as pl
+from jax.experimental.pallas import tpu as pltpu
 from jax.sharding import PartitionSpec as P
 
 S = 1024
@@ -12,6 +14,51 @@
 
 
 HIGHEST = lax.Precision.HIGHEST
+HIGH = lax.Precision.HIGH
+TILE = 8
+
+
+def _kernel(a_ref, l_ref, x_ref, t_ref):
+    n = a_ref.shape[0]
+    tiles = n // TILE
+    row = lax.broadcasted_iota(jnp.int32, (n, n), 0)
+    col = lax.broadcasted_iota(jnp.int32, (n, n), 1)
+    a = a_ref[...]
+    t_ref[...] = jnp.where(row >= col, a, a.T)
+    work = [t_ref[b * TILE : (b + 1) * TILE, :] for b in range(tiles)]
+    sub = lax.broadcasted_iota(jnp.int32, (TILE, n), 0)
+    lane = lax.broadcasted_iota(jnp.int32, (TILE, n), 1)
+    lane1 = lax.broadcasted_iota(jnp.int32, (1, n), 1)
+    sub1 = lax.broadcasted_iota(jnp.int32, (TILE, 1), 0)
+    inv = [jnp.where(lane == sub + b * TILE, 1.0, 0.0).astype(jnp.float32) for b in range(tiles)]
+    for c in range(n):
+        first, i = divmod(c, TILE)
+        ri = work[first][i : i + 1, :]
+        s = lax.rsqrt(ri[:, c : c + 1])
+        li = jnp.where(lane1 >= c, ri * s, 0.0)
+        t_ref[c : c + 1, :] = li
+        xi = inv[first][i : i + 1, :] * s
+        for b in range(first, tiles):
+            lk = work[b][:, c : c + 1] * s
+            if b == first:
+                lk = jnp.where(sub1 > i, lk, 0.0)
+            work[b] = work[b] - lk * li
+            if b == first:
+                inv[b] = jnp.where(sub == i, xi, inv[b] - lk * xi)
+            else:
+                inv[b] = inv[b] - lk * xi
+    for b in range(tiles):
+        x_ref[b * TILE : (b + 1) * TILE, :] = inv[b]
+    l_ref[...] = t_ref[...].T
+
+
+def base_cholesky_inverse(a):
+    n = a.shape[0]
+    return pl.pallas_call(
+        _kernel,
+        out_shape=(jax.ShapeDtypeStruct((n, n), jnp.float32), jax.ShapeDtypeStruct((n, n), jnp.float32)),
+        scratch_shapes=[pltpu.VMEM((n, n), jnp.float32)],
+    )(a)
 
 
 def partner_2(block, axis, bit):
@@ -93,18 +140,16 @@
 def cholesky_inverse(matrix, base_size):
     order = matrix.shape[0]
     if order <= base_size:
-        lower = jnp.linalg.cholesky(matrix)
-        identity = jnp.eye(order, dtype=jnp.float32)
-        return (lower, jax.scipy.linalg.solve_triangular(lower, identity, lower=True))
+        return base_cholesky_inverse(matrix)
     half = order // 2
     lower_11, inverse_11 = cholesky_inverse(matrix[:half, :half], base_size)
-    lower_21 = jnp.dot(matrix[half:, :half], inverse_11.T, precision=HIGHEST, preferred_element_type=jnp.float32)
-    schur = matrix[half:, half:] - jnp.dot(lower_21, lower_21.T, precision=HIGHEST, preferred_element_type=jnp.float32)
+    lower_21 = jnp.dot(matrix[half:, :half], inverse_11.T, precision=HIGH, preferred_element_type=jnp.float32)
+    schur = matrix[half:, half:] - jnp.dot(lower_21, lower_21.T, precision=HIGH, preferred_element_type=jnp.float32)
     lower_22, inverse_22 = cholesky_inverse(schur, base_size)
     inverse_21 = -jnp.dot(
         inverse_22,
-        jnp.dot(lower_21, inverse_11, precision=HIGHEST, preferred_element_type=jnp.float32),
-        precision=HIGHEST,
+        jnp.dot(lower_21, inverse_11, precision=HIGH, preferred_element_type=jnp.float32),
+        precision=HIGH,
         preferred_element_type=jnp.float32,
     )
     zero = jnp.zeros((half, half), jnp.float32)
@@ -164,7 +209,9 @@
         0, row_count // step_rows, add_rows, jnp.zeros((target_total, BLK, BLK), jnp.float32)
     )
     per_front = gram_blocks.reshape(front_total, S, BLK)
-    obs_share = lax.psum(lax.psum_scatter(per_front, "inner", scatter_dimension=1, tiled=True), "outer")
+    obs_share = lax.psum_scatter(per_front, "inner", scatter_dimension=1, tiled=True)
+    for bit in range(group_count.bit_length() - 1):
+        obs_share = obs_share + partner_2(obs_share, "outer", bit)
     current = child_update[0]
     pivot_list = []
     border_list = []
@@ -197,14 +244,14 @@
         coupling_all = lax.all_gather(border_front[:, :S], "inner", axis=0, tiled=True)
         pivot_lower, pivot_inverse = cholesky_inverse(pivot_all, BLK)
         border_all = jnp.dot(
-            coupling_all, pivot_inverse.T, precision=HIGHEST, preferred_element_type=jnp.float32
+            coupling_all, pivot_inverse.T, precision=HIGH, preferred_element_type=jnp.float32
         )
         border_factor = lax.dynamic_slice_in_dim(border_all, member * (B // inner_count), B // inner_count, 0)
         product = jnp.einsum(
             "rs,cs->rc",
             border_factor,
             border_all,
-            precision=HIGHEST,
+            precision=HIGH,
             preferred_element_type=jnp.float32,
         )
         current = border_front[:, S:] - product

time: 1060 us -> 731 us (0.69)
  other arithmetic: 460 us -> 47.3 us
  Pallas kernels: 0 us -> 198 us
  blocking collectives: 42.2 us -> 0 us
  matrix products: 169 us -> 130 us
  local copies, waits for them, and re-layouts: 113 us -> 85.2 us
  waiting for transfers between devices: 241 us -> 222 us
  starting transfers between devices: 10.3 us -> 21.8 us
    another operation x80 -> x0, other arithmetic: 406 us -> none  [the longest x48 214 us: cholesky_inverse(): lower = jnp.linalg.cholesky(matrix)]
    pallas_call x0 -> x16, Pallas kernels: none -> 198 us  [base_cholesky_inverse(): pl.pallas_call(_kernel, out_shape=(jax.ShapeDtypeStruct((n, n), jnp.float...]
    psum x1 -> x0, waiting for transfers between devices: 58.8 us -> none  [shards(): lax.psum(lax.psum_scatter(per_front, 'inner', scatter_dimension=1, tiled=...]
    reduce_scatter x1, waiting for transfers between devices: 39.4 us -> 83.3 us  [shards(): lax.psum_scatter(per_front, 'inner', scatter_dimension=1, tiled=True)]
    all_to_all x1 -> x0, blocking collectives: 42.2 us -> none  [shards(): lax.all_to_all(outgoing, 'inner', split_axis=2, concat_axis=1, tiled=True)]
    dot_general x60, matrix products: 144 us -> 119 us  [the longest x2 40.5 us: shards(): jnp.dot(coupling_all, pivot_inverse.T, precision=HIGH, preferred_element_...]
    another operation x16 -> x0, matrix products: 12.9 us -> none  [cholesky_inverse(): jax.scipy.linalg.solve_triangular(lower, identity, lower=True)]
    div x14 -> x0, other arithmetic: 11.4 us -> none  [cholesky_inverse(): lower = jnp.linalg.cholesky(matrix)]
  transfers between devices with their start and end apart: 9 -> 12, of which waited for: 6 -> 8; matrix products, arithmetic and copies ran while one was open for 59% -> 22% of each run, Pallas kernels for 0% -> 27%
where the time goes in v4:
time: 731 us; the launch traced here: 720 us
  waiting for transfers between devices  222 us (30%)
  Pallas kernels  198 us (27%)
  matrix products  130 us (18%)
  local copies, waits for them, and re-layouts  85.2 us (12%)
  other arithmetic  47.3 us (6%)
  starting transfers between devices  21.8 us (3%)
  between operations  16 us (2%)
    pallas_call x16, Pallas kernels, base_cholesky_inverse(): pl.pallas_call(_kernel, out_shape=(jax.ShapeDtypeStruct((n, n), jnp.float...  198 us
    reduce_scatter x1, waiting for transfers between devices, shards(): lax.psum_scatter(per_front, 'inner', scatter_dimension=1, tiled=True)  83.3 us
    all_gather x2, waiting for transfers between devices, shards(): pivot_all = lax.all_gather(sep_front[:, :S], 'inner', axis=0, tiled=True)  82.1 us
    dot_general x2, matrix products, shards(): jnp.dot(coupling_all, pivot_inverse.T, precision=HIGH, preferred_element_...  40.5 us
    all_to_all x2, waiting for transfers between devices, shards(): lax.all_to_all(outgoing, 'inner', split_axis=2, concat_axis=1, tiled=True)  37.4 us
    dot_general x14, matrix products, cholesky_inverse(): jnp.dot(lower_21, lower_21.T, precision=HIGH, preferred_element_type=jnp....  23.1 us
    dot_general x14, matrix products, cholesky_inverse(): jnp.dot(matrix[half:, :half], inverse_11.T, precision=HIGH, preferred_ele...  19.2 us
    ppermute x5, waiting for transfers between devices, partner_2(): return lax.ppermute(block, axis, route)  18.6 us
  transfers between devices with their start and end apart: 12, of which 8 were waited for; matrix products, arithmetic and copies ran while one was open for 22% of the time, Pallas kernels for 27%

profile of v4, /device:TPU:1, one launch (start us, length us, event | category | flops | bytes accessed | tf_op | source)
XLA Modules:
  0.0 720.5 jit_solution(7223423020034137283)
XLA Ops:
  7.2 25.9 %while.14 = (s32[]{:T(128)}, f32[48,128,128]{2,1,0:T(8,128)S(1)}, s32[2048]{0:T(1024)}, bf16[2048,128]{1,0:T(8,128)(2,1)}, s32[]{:T(128)}, /*index=5*/s32[]{:T(128)}, s32[]{:T(128)}, s32[]{:T(128)}) while((s32[]{:T(128)}, f32[48,128,128]{2,1,0:T(8,128)S(1)}, s32[2048]{0:T(1024)}, bf16[2048,128]{1,0:T(8,128)(2,1)}, s32[]{:T(128)}, ...), condition=%wide.region_5.8_spmd.clone, body=%wide.region_4.7_spmd.clone.sunk | while | flops 405823488 | bytes 6737053 | solution.py:208
  63.0 83.3 %reduce-scatter.2.cloned.1.call-done = f32[6,64,128]{2,1,0:T(8,128)} async-done(((f32[6,1024,128]{2,1,0:T(8,128)}), f32[6,64,128]{2,1,0:T(8,128)}) %reduce-scatter.2.cloned.1.call-update) | async-done | bytes 196624 | tf_op jit(solution)/shard_map/reduce_scatter | solution.py:212
  167.4 50.1 %all-gather.5.cloned.1.call-done = f32[1024,1024]{1,0:T(8,128)} async-done(((f32[64,1024]{1,0:T(8,128)}), f32[1024,1024]{1,0:T(8,128)}) %all-gather.5.cloned.1.call-update) | async-done | bytes 4194320 | tf_op jit(solution)/shard_map/all_gather | solution.py:242
  218.9 12.3 %shard_map.67 = (f32[128,128]{1,0:T(8,128)}, f32[128,128]{1,0:T(8,128)}) custom-call(f32[128,128]{1,0:T(8,128)} %slice.290.a_ref), custom_call_target="tpu_custom_call" | custom-call | tf_op jit(solution)/shard_map/pallas_call | solution.py:57
  234.1 12.3 %shard_map.68 = (f32[128,128]{1,0:T(8,128)}, f32[128,128]{1,0:T(8,128)}) custom-call(f32[128,128]{1,0:T(8,128)} %convolution_subtract_fusion.15.a_ref), custom_call_target="tpu_custom_call" | custom-call | tf_op jit(solution)/shard_map/pallas_call | solution.py:57
  251.9 12.7 %shard_map.69 = (f32[128,128]{1,0:T(8,128)}, f32[128,128]{1,0:T(8,128)}) custom-call(f32[128,128]{1,0:T(8,128)} %slice.295.a_ref), custom_call_target="tpu_custom_call" | custom-call | tf_op jit(solution)/shard_map/pallas_call | solution.py:57
  267.4 12.3 %shard_map.70 = (f32[128,128]{1,0:T(8,128)}, f32[128,128]{1,0:T(8,128)}) custom-call(f32[128,128]{1,0:T(8,128)} %convolution_subtract_fusion.14.a_ref), custom_call_target="tpu_custom_call" | custom-call | tf_op jit(solution)/shard_map/pallas_call | solution.py:57
  291.6 12.5 %shard_map.71 = (f32[128,128]{1,0:T(8,128)}, f32[128,128]{1,0:T(8,128)}) custom-call(f32[128,128]{1,0:T(8,128)} %slice.300.a_ref), custom_call_target="tpu_custom_call" | custom-call | tf_op jit(solution)/shard_map/pallas_call | solution.py:57
  307.5 12.3 %shard_map.72 = (f32[128,128]{1,0:T(8,128)}, f32[128,128]{1,0:T(8,128)}) custom-call(f32[128,128]{1,0:T(8,128)} %convolution_subtract_fusion.13.a_ref), custom_call_target="tpu_custom_call" | custom-call | tf_op jit(solution)/shard_map/pallas_call | solution.py:57
  326.6 12.5 %shard_map.73 = (f32[128,128]{1,0:T(8,128)}, f32[128,128]{1,0:T(8,128)}) custom-call(f32[128,128]{1,0:T(8,128)} %slice.305.a_ref), custom_call_target="tpu_custom_call" | custom-call | tf_op jit(solution)/shard_map/pallas_call | solution.py:57
  344.1 12.3 %shard_map.74 = (f32[128,128]{1,0:T(8,128)}, f32[128,128]{1,0:T(8,128)}) custom-call(f32[128,128]{1,0:T(8,128)} %convolution_subtract_fusion.12.a_ref), custom_call_target="tpu_custom_call" | custom-call | tf_op jit(solution)/shard_map/pallas_call | solution.py:57
  365.2 23.7 %fusion.12 = f32[2048,1024]{1,0:T(8,128)S(1)} fusion(f32[2048,1024]{1,0:T(8,128)} %all-gather.7.cloned.1.call-done, f32[512,512]{1,0:T(8,128)S(1)} %copy-done.36, f32[128,128]{1,0:T(8,128)} %get-tuple-element.147, f32[128,128]{1,0:T(8,128)} %copy-done.69, f32[128,256]{1,0:T(8,128)} %concatenate.310, f32[256,256]{1,0:T(8,128)} %copy-done.65, ...), kind=kOutput, calls=%fused_computation.29 | convolution fusion | flops 12893290496 | bytes 19922944 | tf_op jit(solution)/shard_map/dot_general | solution.py:246
  402.4 16.2 %collective-permute-done.4 = f32[128,2048]{1,0:T(8,128)} collective-permute-done((f32[128,2048]{1,0:T(8,128)}, f32[128,2048]{1,0:T(8,128)}, u32[]{:S(2)}, u32[]{:S(2)}) %collective-permute-start.4) | collective-permute-done | bytes 1048608 | tf_op jit(solution)/shard_map/ppermute | solution.py:71
  432.2 37.4 %all-to-all-done.1 = f32[2,128,16,192]{1,3,0,2:T(8,128)S(1)} async-done(((f32[2,128,16,192]{1,3,0,2:T(8,128)}), f32[2,128,16,192]{1,3,0,2:T(8,128)S(1)}, u32[]{:S(2)}, u32[]{:S(2)}) %all-to-all-start.1) | async-done | bytes 3145760 | tf_op jit(solution)/shard_map/all_to_all | solution.py:232
  501.8 32.0 %all-gather.9.cloned.1.call-done = f32[1024,1024]{1,0:T(8,128)} async-done(((f32[64,1024]{1,0:T(8,128)}), f32[1024,1024]{1,0:T(8,128)}) %all-gather.9.cloned.1.call-update) | async-done | bytes 4194320 | tf_op jit(solution)/shard_map/all_gather | solution.py:242
  535.3 12.3 %shard_map.75 = (f32[128,128]{1,0:T(8,128)}, f32[128,128]{1,0:T(8,128)}) custom-call(f32[128,128]{1,0:T(8,128)} %slice.318.a_ref), custom_call_target="tpu_custom_call" | custom-call | tf_op jit(solution)/shard_map/pallas_call | solution.py:57
  551.1 12.3 %shard_map.76 = (f32[128,128]{1,0:T(8,128)}, f32[128,128]{1,0:T(8,128)}) custom-call(f32[128,128]{1,0:T(8,128)} %convolution_subtract_fusion.11.a_ref), custom_call_target="tpu_custom_call" | custom-call | tf_op jit(solution)/shard_map/pallas_call | solution.py:57
  570.1 12.3 %shard_map.77 = (f32[128,128]{1,0:T(8,128)}, f32[128,128]{1,0:T(8,128)}) custom-call(f32[128,128]{1,0:T(8,128)} %slice.323.a_ref), custom_call_target="tpu_custom_call" | custom-call | tf_op jit(solution)/shard_map/pallas_call | solution.py:57
  586.0 12.3 %shard_map.78 = (f32[128,128]{1,0:T(8,128)}, f32[128,128]{1,0:T(8,128)}) custom-call(f32[128,128]{1,0:T(8,128)} %convolution_subtract_fusion.10.a_ref), custom_call_target="tpu_custom_call" | custom-call | tf_op jit(solution)/shard_map/pallas_call | solution.py:57
  610.4 12.3 %shard_map.79 = (f32[128,128]{1,0:T(8,128)}, f32[128,128]{1,0:T(8,128)}) custom-call(f32[128,128]{1,0:T(8,128)} %slice.328.a_ref), custom_call_target="tpu_custom_call" | custom-call | tf_op jit(solution)/shard_map/pallas_call | solution.py:57
  626.2 12.3 %shard_map.80 = (f32[128,128]{1,0:T(8,128)}, f32[128,128]{1,0:T(8,128)}) custom-call(f32[128,128]{1,0:T(8,128)} %convolution_subtract_fusion.9.a_ref), custom_call_target="tpu_custom_call" | custom-call | tf_op jit(solution)/shard_map/pallas_call | solution.py:57
  647.3 12.5 %shard_map.81 = (f32[128,128]{1,0:T(8,128)}, f32[128,128]{1,0:T(8,128)}) custom-call(f32[128,128]{1,0:T(8,128)} %slice.333.a_ref), custom_call_target="tpu_custom_call" | custom-call | tf_op jit(solution)/shard_map/pallas_call | solution.py:57
  664.8 12.3 %shard_map.82 = (f32[128,128]{1,0:T(8,128)}, f32[128,128]{1,0:T(8,128)}) custom-call(f32[128,128]{1,0:T(8,128)} %convolution_subtract_fusion.8.a_ref), custom_call_target="tpu_custom_call" | custom-call | tf_op jit(solution)/shard_map/pallas_call | solution.py:57
  690.2 16.8 %fusion.10 = f32[2048,1024]{1,0:T(8,128)S(1)} fusion(f32[2048,1024]{1,0:T(8,128)} %all-gather.11.cloned.1.call-done, f32[512,512]{1,0:T(8,128)S(1)} %copy-done.35, f32[128,128]{1,0:T(8,128)} %get-tuple-element.163, f32[128,128]{1,0:T(8,128)} %copy-done.68, f32[128,256]{1,0:T(8,128)S(1)} %copy-done.59, f32[256,256]{1,0:T(8,128)} %copy-done.64, ...), kind=kOutput, calls=%fused_computation.23 | convolution fusion | flops 12893290496 | bytes 19922944 | tf_op jit(solution)/shard_map/dot_general | solution.py:246
  (418 shorter events, 246.9 us)
Async XLA Ops:
  7.2 139.1 %reduce-scatter.2.cloned.1.call-start = ((), (), s32[]{:S(2)}) async-start(), calls=%async_computation.3 | async-start | bytes 3342336 | tf_op jit(solution)/shard_map/reduce_scatter | solution.py:212
  37.4 9.8 %collective-permute-start = (f32[128,2048]{0,1:T(8,128)}, f32[128,2048]{0,1:T(8,128)}, u32[]{:S(2)}, u32[]{:S(2)}) collective-permute-start(f32[128,2048]{0,1:T(8,128)} %bitcast.8), channel_id=1, source_target_pairs={{0,16},{16,0},{32,48},{48,32},{64,80},{80,64},{96,112},{112,96},{1... | collective-permute-start | bytes 3145736 | tf_op jit(solution)/shard_map/ppermute | solution.py:71
  56.0 92.6 %all-to-all-start = ((f32[2,128,16,192]{1,3,0,2:T(8,128)}), f32[2,128,16,192]{1,3,0,2:T(8,128)S(1)}, u32[]{:S(2)}, u32[]{:S(2)}) async-start(f32[2,128,16,192]{1,3,0,2:T(8,128)} %pad_maximum_fusion), calls=%async_computation | async-start | bytes 6291456 | tf_op jit(solution)/shard_map/all_to_all | solution.py:232
  62.9 154.5 %all-gather.5.cloned.1.call-start = ((), (), s32[]{:S(2)}) async-start(), calls=%async_computation.4 | async-start | bytes 4456448 | tf_op jit(solution)/shard_map/all_gather | solution.py:242
  146.3 3.8 collective-permute-start.1
  151.0 6.2 collective-permute-start.2
  157.2 6.8 collective-permute-start.3
  165.4 199.8 %all-gather.7.cloned.1.call-start = ((), (), s32[]{:S(2)}) async-start(), calls=%async_computation.5 | async-start | bytes 8912896 | tf_op jit(solution)/shard_map/all_gather | solution.py:244
  231.2 48.5 %copy-start.21 = (f32[128,128]{1,0:T(8,128)S(1)}, f32[128,128]{1,0:T(8,128)}, u32[]{:S(2)}) copy-start(f32[128,128]{1,0:T(8,128)} %get-tuple-element.133) | copy-start | bytes 196612
  246.4 36.4 %copy-start.44 = (f32[128,128]{1,0:T(8,128)S(1)}, f32[128,128]{1,0:T(8,128)}, u32[]{:S(2)}) copy-start(f32[128,128]{1,0:T(8,128)} %get-tuple-element.135) | copy-start | bytes 196612
  249.8 33.4 %copy-start.4 = (f32[256,256]{0,1:T(8,128)}, f32[256,256]{0,1:T(8,128)S(1)}, u32[]{:S(2)}) copy-start(f32[256,256]{0,1:T(8,128)S(1)} %fusion.101) | copy-start | bytes 786436
  265.4 17.8 %copy-start.24 = (f32[128,256]{1,0:T(8,128)}, f32[128,256]{1,0:T(8,128)S(1)}, u32[]{:S(2)}) copy-start(f32[128,256]{1,0:T(8,128)S(1)} %concatenate.289) | copy-start | bytes 393220
  287.4 74.7 %copy-start.2 = (f32[512,512]{0,1:T(8,128)}, f32[512,512]{0,1:T(8,128)S(1)}, u32[]{:S(2)}) copy-start(f32[512,512]{0,1:T(8,128)S(1)} %fusion.51) | copy-start | bytes 3145732
  394.4 24.2 %collective-permute-start.4 = (f32[128,2048]{1,0:T(8,128)}, f32[128,2048]{1,0:T(8,128)}, u32[]{:S(2)}, u32[]{:S(2)}) collective-permute-start(f32[128,2048]{1,0:T(8,128)} %convolution_subtract_fusion.1), channel_id=1, source_target_pairs={{0,32},{32,0},{16,48},{48,16},{64,96},{96,64},{80,112},{112,80},{1... | collective-permute-start | bytes 3145736 | tf_op jit(solution)/shard_map/ppermute | solution.py:71
  427.1 42.5 %all-to-all-start.1 = ((f32[2,128,16,192]{1,3,0,2:T(8,128)}), f32[2,128,16,192]{1,3,0,2:T(8,128)S(1)}, u32[]{:S(2)}, u32[]{:S(2)}) async-start(f32[2,128,16,192]{1,3,0,2:T(8,128)} %pad_maximum_fusion.1), calls=%async_computation.2 | async-start | bytes 6291456 | tf_op jit(solution)/shard_map/all_to_all | solution.py:232
  432.1 101.7 %all-gather.9.cloned.1.call-start = ((), (), s32[]{:S(2)}) async-start(), calls=%async_computation.6 | async-start | bytes 4456448 | tf_op jit(solution)/shard_map/all_gather | solution.py:242
  478.7 11.8 %copy-start.3 = (f32[512,512]{0,1:T(8,128)S(1)}, f32[512,512]{0,1:T(8,128)}, u32[]{:S(2)}) copy-start(f32[512,512]{0,1:T(8,128)} %copy-done.2) | copy-start | bytes 3145732
  478.7 211.4 %all-gather.11.cloned.1.call-start = ((), (), s32[]{:S(2)}) async-start(), calls=%async_computation.7 | async-start | bytes 8912896 | tf_op jit(solution)/shard_map/all_gather | solution.py:244
  547.6 50.7 %copy-start.19 = (f32[128,128]{1,0:T(8,128)S(1)}, f32[128,128]{1,0:T(8,128)}, u32[]{:S(2)}) copy-start(f32[128,128]{1,0:T(8,128)} %get-tuple-element.149) | copy-start | bytes 196612
  563.5 34.8 %copy-start.43 = (f32[128,128]{1,0:T(8,128)S(1)}, f32[128,128]{1,0:T(8,128)}, u32[]{:S(2)}) copy-start(f32[128,128]{1,0:T(8,128)} %get-tuple-element.151) | copy-start | bytes 196612
  583.3 21.7 %copy-start.22 = (f32[128,256]{1,0:T(8,128)}, f32[128,256]{1,0:T(8,128)S(1)}, u32[]{:S(2)}) copy-start(f32[128,256]{1,0:T(8,128)S(1)} %concatenate.333) | copy-start | bytes 393220
  622.7 54.5 %copy-start.18 = (f32[128,128]{1,0:T(8,128)S(1)}, f32[128,128]{1,0:T(8,128)}, u32[]{:S(2)}) copy-start(f32[128,128]{1,0:T(8,128)} %get-tuple-element.157) | copy-start | bytes 196612
  640.6 19.2 %copy-start.40 = (f32[128,128]{1,0:T(8,128)}, f32[128,128]{1,0:T(8,128)S(1)}, u32[]{:S(2)}) copy-start(f32[128,128]{1,0:T(8,128)S(1)} %convolution_negate_fusion.7) | copy-start | bytes 196612
  678.1 10.0 %copy-start.56 = (f32[256,512]{1,0:T(8,128)}, f32[256,512]{1,0:T(8,128)S(1)}, u32[]{:S(2)}) copy-start(f32[256,512]{1,0:T(8,128)S(1)} %concatenate.353) | copy-start | bytes 1572868
  (75 other events, 238.5 us)
Sparse Core Ops, SparseCore 0:
  35.0 111.2 reduce-scatter.1
  165.5 51.8 all-gather.4
  220.1 70.5 all-gather.6
  478.8 54.9 all-gather.8
  535.8 70.4 all-gather.10

commit v5 on v4

--- a/solution.py
+++ b/solution.py
@@ -242,17 +242,39 @@
         pivot_all = lax.all_gather(sep_front[:, :S], "inner", axis=0, tiled=True)
         border_front = front_rows[sep_rows:]
         coupling_all = lax.all_gather(border_front[:, :S], "inner", axis=0, tiled=True)
-        pivot_lower, pivot_inverse = cholesky_inverse(pivot_all, BLK)
-        border_all = jnp.dot(
-            coupling_all, pivot_inverse.T, precision=HIGH, preferred_element_type=jnp.float32
-        )
-        border_factor = lax.dynamic_slice_in_dim(border_all, member * (B // inner_count), B // inner_count, 0)
-        product = jnp.einsum(
-            "rs,cs->rc",
-            border_factor,
-            border_all,
+        half = S // 2
+        lower_11, inverse_11 = cholesky_inverse(pivot_all[:half, :half], BLK)
+        lower_21 = jnp.dot(
+            pivot_all[half:, :half], inverse_11.T, precision=HIGH, preferred_element_type=jnp.float32
+        )
+        schur = pivot_all[half:, half:] - jnp.dot(
+            lower_21, lower_21.T, precision=HIGH, preferred_element_type=jnp.float32
+        )
+        lower_22, inverse_22 = cholesky_inverse(schur, BLK)
+        inverse_21 = -jnp.dot(
+            inverse_22,
+            jnp.dot(lower_21, inverse_11, precision=HIGH, preferred_element_type=jnp.float32),
             precision=HIGH,
             preferred_element_type=jnp.float32,
+        )
+        zero = jnp.zeros((half, half), jnp.float32)
+        pivot_lower = jnp.block([[lower_11, zero], [lower_21, lower_22]])
+        border_left = jnp.dot(
+            coupling_all[:, :half], inverse_11.T, precision=HIGH, preferred_element_type=jnp.float32
+        )
+        border_right = jnp.dot(
+            coupling_all[:, :half], inverse_21.T, precision=HIGH, preferred_element_type=jnp.float32
+        ) + jnp.dot(
+            coupling_all[:, half:], inverse_22.T, precision=HIGH, preferred_element_type=jnp.float32
+        )
+        own_rows = B // inner_count
+        own_left = lax.dynamic_slice_in_dim(border_left, member * own_rows, own_rows, 0)
+        own_right = lax.dynamic_slice_in_dim(border_right, member * own_rows, own_rows, 0)
+        border_factor = jnp.concatenate([own_left, own_right], axis=1)
+        product = jnp.einsum(
+            "rs,cs->rc", own_left, border_left, precision=HIGH, preferred_element_type=jnp.float32
+        ) + jnp.einsum(
+            "rs,cs->rc", own_right, border_right, precision=HIGH, preferred_element_type=jnp.float32
         )
         current = border_front[:, S:] - product
         pivot_list.append(lax.dynamic_slice_in_dim(pivot_lower, member * sep_rows, sep_rows, 0))

time: 731 us -> 714 us (0.977)
  matrix products: 130 us -> 115 us
    dot_general x14 -> x12, matrix products: 23.1 us -> 17.8 us  [cholesky_inverse(): jnp.dot(lower_21, lower_21.T, precision=HIGH, preferred_element_type=jnp....]
    dot_general x14 -> x12, matrix products: 19.2 us -> 14.6 us  [cholesky_inverse(): jnp.dot(matrix[half:, :half], inverse_11.T, precision=HIGH, preferred_ele...]
    dot_general x14 -> x12, local copies, waits for them, and re-layouts: 15.6 us -> 13.1 us  [cholesky_inverse(): jnp.dot(matrix[half:, :half], inverse_11.T, precision=HIGH, preferred_ele...]
    unnamed x175 -> x208, local copies, waits for them, and re-layouts: 14.1 us -> 16.3 us
    dot_general x4 -> x18, matrix products: 51.3 us -> 49.5 us  [the longest x2 9.23 us: shards(): jnp.dot(coupling_all[:, half:], inverse_22.T, precision=HIGH, preferred_e...]
  transfers between devices with their start and end apart: 12 -> 12, of which waited for: 8 -> 8; matrix products, arithmetic and copies ran while one was open for 22% -> 22% of each run, Pallas kernels for 27% -> 28%
where the time goes in v5:
time: 714 us; the launch traced here: 703 us
  waiting for transfers between devices  221 us (31%)
  Pallas kernels  198 us (28%)
  matrix products  115 us (16%)
  local copies, waits for them, and re-layouts  85.5 us (12%)
  other arithmetic  43.7 us (6%)
  starting transfers between devices  22.2 us (3%)
  between operations  16.1 us (2%)
    pallas_call x16, Pallas kernels, base_cholesky_inverse(): pl.pallas_call(_kernel, out_shape=(jax.ShapeDtypeStruct((n, n), jnp.float...  198 us
    reduce_scatter x1, waiting for transfers between devices, shards(): lax.psum_scatter(per_front, 'inner', scatter_dimension=1, tiled=True)  82.7 us
    all_gather x2, waiting for transfers between devices, shards(): pivot_all = lax.all_gather(sep_front[:, :S], 'inner', axis=0, tiled=True)  82.7 us
    all_to_all x2, waiting for transfers between devices, shards(): lax.all_to_all(outgoing, 'inner', split_axis=2, concat_axis=1, tiled=True)  37.4 us
    ppermute x5, waiting for transfers between devices, partner_2(): return lax.ppermute(block, axis, route)  18.6 us
    dot_general x12, matrix products, cholesky_inverse(): jnp.dot(lower_21, lower_21.T, precision=HIGH, preferred_element_type=jnp....  17.8 us
    unnamed x208, local copies, waits for them, and re-layouts  16.3 us
    concatenate x10, other arithmetic, cholesky_inverse(): lower = jnp.block([[lower_11, zero], [lower_21, lower_22]])  15.2 us
  transfers between devices with their start and end apart: 12, of which 8 were waited for; matrix products, arithmetic and copies ran while one was open for 22% of the time, Pallas kernels for 28%

profile of v5, /device:TPU:1, one launch (start us, length us, event | category | flops | bytes accessed | tf_op | source)
XLA Modules:
  0.0 703.0 jit_solution(4213207551826060706)
XLA Ops:
  7.2 26.0 %while.14 = (s32[]{:T(128)}, f32[48,128,128]{2,1,0:T(8,128)S(1)}, s32[2048]{0:T(1024)}, bf16[2048,128]{1,0:T(8,128)(2,1)}, s32[]{:T(128)}, /*index=5*/s32[]{:T(128)}, s32[]{:T(128)}, s32[]{:T(128)}) while((s32[]{:T(128)}, f32[48,128,128]{2,1,0:T(8,128)S(1)}, s32[2048]{0:T(1024)}, bf16[2048,128]{1,0:T(8,128)(2,1)}, s32[]{:T(128)}, ...), condition=%wide.region_5.8_spmd.clone, body=%wide.region_4.7_spmd.clone.sunk | while | flops 405823488 | bytes 6737045 | solution.py:208
  55.9 6.9 all-to-all-start
  62.8 82.7 %reduce-scatter.2.cloned.1.call-done = f32[6,64,128]{2,1,0:T(8,128)} async-done(((f32[6,1024,128]{2,1,0:T(8,128)}), f32[6,64,128]{2,1,0:T(8,128)}) %reduce-scatter.2.cloned.1.call-update) | async-done | bytes 196624 | tf_op jit(solution)/shard_map/reduce_scatter | solution.py:212
  166.8 49.9 %all-gather.5.cloned.1.call-done = f32[1024,1024]{1,0:T(8,128)} async-done(((f32[64,1024]{1,0:T(8,128)}), f32[1024,1024]{1,0:T(8,128)}) %all-gather.5.cloned.1.call-update) | async-done | bytes 4194320 | tf_op jit(solution)/shard_map/all_gather | solution.py:242
  218.1 12.3 %shard_map.67 = (f32[128,128]{1,0:T(8,128)}, f32[128,128]{1,0:T(8,128)}) custom-call(f32[128,128]{1,0:T(8,128)} %slice.308.a_ref), custom_call_target="tpu_custom_call" | custom-call | tf_op jit(solution)/shard_map/pallas_call | solution.py:57
  233.3 12.3 %shard_map.68 = (f32[128,128]{1,0:T(8,128)}, f32[128,128]{1,0:T(8,128)}) custom-call(f32[128,128]{1,0:T(8,128)} %convolution_subtract_fusion.13.a_ref), custom_call_target="tpu_custom_call" | custom-call | tf_op jit(solution)/shard_map/pallas_call | solution.py:57
  251.2 12.5 %shard_map.69 = (f32[128,128]{1,0:T(8,128)}, f32[128,128]{1,0:T(8,128)}) custom-call(f32[128,128]{1,0:T(8,128)} %slice.313.a_ref), custom_call_target="tpu_custom_call" | custom-call | tf_op jit(solution)/shard_map/pallas_call | solution.py:57
  265.6 12.3 %shard_map.70 = (f32[128,128]{1,0:T(8,128)}, f32[128,128]{1,0:T(8,128)}) custom-call(f32[128,128]{1,0:T(8,128)} %convolution_subtract_fusion.12.a_ref), custom_call_target="tpu_custom_call" | custom-call | tf_op jit(solution)/shard_map/pallas_call | solution.py:57
  290.7 12.5 %shard_map.71 = (f32[128,128]{1,0:T(8,128)}, f32[128,128]{1,0:T(8,128)}) custom-call(f32[128,128]{1,0:T(8,128)} %slice.318.a_ref), custom_call_target="tpu_custom_call" | custom-call | tf_op jit(solution)/shard_map/pallas_call | solution.py:57
  306.6 12.3 %shard_map.72 = (f32[128,128]{1,0:T(8,128)}, f32[128,128]{1,0:T(8,128)}) custom-call(f32[128,128]{1,0:T(8,128)} %convolution_subtract_fusion.11.a_ref), custom_call_target="tpu_custom_call" | custom-call | tf_op jit(solution)/shard_map/pallas_call | solution.py:57
  325.8 12.7 %shard_map.73 = (f32[128,128]{1,0:T(8,128)}, f32[128,128]{1,0:T(8,128)}) custom-call(f32[128,128]{1,0:T(8,128)} %slice.323.a_ref), custom_call_target="tpu_custom_call" | custom-call | tf_op jit(solution)/shard_map/pallas_call | solution.py:57
  343.5 12.3 %shard_map.74 = (f32[128,128]{1,0:T(8,128)}, f32[128,128]{1,0:T(8,128)}) custom-call(f32[128,128]{1,0:T(8,128)} %convolution_subtract_fusion.10.a_ref), custom_call_target="tpu_custom_call" | custom-call | tf_op jit(solution)/shard_map/pallas_call | solution.py:57
  366.1 5.7 fusion.12
  391.5 16.1 %collective-permute-done.4 = f32[128,2048]{1,0:T(8,128)} collective-permute-done((f32[128,2048]{1,0:T(8,128)}, f32[128,2048]{1,0:T(8,128)}, u32[]{:S(2)}, u32[]{:S(2)}) %collective-permute-start.4) | collective-permute-done | bytes 1048608 | tf_op jit(solution)/shard_map/ppermute | solution.py:71
  421.2 37.4 %all-to-all-done.1 = f32[2,128,16,192]{1,3,0,2:T(8,128)S(1)} async-done(((f32[2,128,16,192]{1,3,0,2:T(8,128)}), f32[2,128,16,192]{1,3,0,2:T(8,128)S(1)}, u32[]{:S(2)}, u32[]{:S(2)}) %all-to-all-start.1) | async-done | bytes 3145760 | tf_op jit(solution)/shard_map/all_to_all | solution.py:232
  490.1 32.8 %all-gather.9.cloned.1.call-done = f32[1024,1024]{1,0:T(8,128)} async-done(((f32[64,1024]{1,0:T(8,128)}), f32[1024,1024]{1,0:T(8,128)}) %all-gather.9.cloned.1.call-update) | async-done | bytes 4194320 | tf_op jit(solution)/shard_map/all_gather | solution.py:242
  524.4 12.3 %shard_map.75 = (f32[128,128]{1,0:T(8,128)}, f32[128,128]{1,0:T(8,128)}) custom-call(f32[128,128]{1,0:T(8,128)} %slice.338.a_ref), custom_call_target="tpu_custom_call" | custom-call | tf_op jit(solution)/shard_map/pallas_call | solution.py:57
  540.3 12.3 %shard_map.76 = (f32[128,128]{1,0:T(8,128)}, f32[128,128]{1,0:T(8,128)}) custom-call(f32[128,128]{1,0:T(8,128)} %convolution_subtract_fusion.9.a_ref), custom_call_target="tpu_custom_call" | custom-call | tf_op jit(solution)/shard_map/pallas_call | solution.py:57
  559.0 12.3 %shard_map.77 = (f32[128,128]{1,0:T(8,128)}, f32[128,128]{1,0:T(8,128)}) custom-call(f32[128,128]{1,0:T(8,128)} %slice.343.a_ref), custom_call_target="tpu_custom_call" | custom-call | tf_op jit(solution)/shard_map/pallas_call | solution.py:57
  574.9 12.3 %shard_map.78 = (f32[128,128]{1,0:T(8,128)}, f32[128,128]{1,0:T(8,128)}) custom-call(f32[128,128]{1,0:T(8,128)} %convolution_subtract_fusion.8.a_ref), custom_call_target="tpu_custom_call" | custom-call | tf_op jit(solution)/shard_map/pallas_call | solution.py:57
  599.5 12.3 %shard_map.79 = (f32[128,128]{1,0:T(8,128)}, f32[128,128]{1,0:T(8,128)}) custom-call(f32[128,128]{1,0:T(8,128)} %slice.348.a_ref), custom_call_target="tpu_custom_call" | custom-call | tf_op jit(solution)/shard_map/pallas_call | solution.py:57
  615.4 12.3 %shard_map.80 = (f32[128,128]{1,0:T(8,128)}, f32[128,128]{1,0:T(8,128)}) custom-call(f32[128,128]{1,0:T(8,128)} %convolution_subtract_fusion.7.a_ref), custom_call_target="tpu_custom_call" | custom-call | tf_op jit(solution)/shard_map/pallas_call | solution.py:57
  636.5 12.7 %shard_map.81 = (f32[128,128]{1,0:T(8,128)}, f32[128,128]{1,0:T(8,128)}) custom-call(f32[128,128]{1,0:T(8,128)} %slice.353.a_ref), custom_call_target="tpu_custom_call" | custom-call | tf_op jit(solution)/shard_map/pallas_call | solution.py:57
  654.3 12.3 %shard_map.82 = (f32[128,128]{1,0:T(8,128)}, f32[128,128]{1,0:T(8,128)}) custom-call(f32[128,128]{1,0:T(8,128)} %convolution_subtract_fusion.6.a_ref), custom_call_target="tpu_custom_call" | custom-call | tf_op jit(solution)/shard_map/pallas_call | solution.py:57
  (456 shorter events, 256.8 us)
Async XLA Ops:
  7.2 138.3 %reduce-scatter.2.cloned.1.call-start = ((), (), s32[]{:S(2)}) async-start(), calls=%async_computation.3 | async-start | bytes 3342336 | tf_op jit(solution)/shard_map/reduce_scatter | solution.py:212
  37.4 9.5 %collective-permute-start = (f32[128,2048]{0,1:T(8,128)}, f32[128,2048]{0,1:T(8,128)}, u32[]{:S(2)}, u32[]{:S(2)}) collective-permute-start(f32[128,2048]{0,1:T(8,128)} %bitcast.8), channel_id=1, source_target_pairs={{0,16},{16,0},{32,48},{48,32},{64,80},{80,64},{96,112},{112,96},{1... | collective-permute-start | bytes 3145736 | tf_op jit(solution)/shard_map/ppermute | solution.py:71
  55.9 92.0 %all-to-all-start = ((f32[2,128,16,192]{1,3,0,2:T(8,128)}), f32[2,128,16,192]{1,3,0,2:T(8,128)S(1)}, u32[]{:S(2)}, u32[]{:S(2)}) async-start(f32[2,128,16,192]{1,3,0,2:T(8,128)} %pad_maximum_fusion), calls=%async_computation | async-start | bytes 6291456 | tf_op jit(solution)/shard_map/all_to_all | solution.py:232
  62.7 153.9 %all-gather.5.cloned.1.call-start = ((), (), s32[]{:S(2)}) async-start(), calls=%async_computation.4 | async-start | bytes 4456448 | tf_op jit(solution)/shard_map/all_gather | solution.py:242
  145.5 3.7 collective-permute-start.1
  150.2 6.2 collective-permute-start.2
  156.4 6.8 collective-permute-start.3
  164.7 201.4 %all-gather.7.cloned.1.call-start = ((), (), s32[]{:S(2)}) async-start(), calls=%async_computation.5 | async-start | bytes 8912896 | tf_op jit(solution)/shard_map/all_gather | solution.py:244
  230.5 48.3 %copy-start.24 = (f32[128,128]{1,0:T(8,128)S(1)}, f32[128,128]{1,0:T(8,128)}, u32[]{:S(2)}) copy-start(f32[128,128]{1,0:T(8,128)} %get-tuple-element.133) | copy-start | bytes 196612
  245.6 36.2 %copy-start.57 = (f32[128,128]{1,0:T(8,128)S(1)}, f32[128,128]{1,0:T(8,128)}, u32[]{:S(2)}) copy-start(f32[128,128]{1,0:T(8,128)} %get-tuple-element.135) | copy-start | bytes 196612
  249.1 33.2 %copy-start.5 = (f32[256,256]{0,1:T(8,128)}, f32[256,256]{0,1:T(8,128)S(1)}, u32[]{:S(2)}) copy-start(f32[256,256]{0,1:T(8,128)S(1)} %fusion.71) | copy-start | bytes 786436
  286.4 75.2 %copy-start.3 = (f32[512,512]{0,1:T(8,128)}, f32[512,512]{0,1:T(8,128)S(1)}, u32[]{:S(2)}) copy-start(f32[512,512]{0,1:T(8,128)S(1)} %fusion.41) | copy-start | bytes 3145732
  355.8 8.2 %copy-start.75 = (f32[128,128]{1,0:T(8,128)S(1)}, f32[128,128]{1,0:T(8,128)}, u32[]{:S(2)}) copy-start(f32[128,128]{1,0:T(8,128)} %get-tuple-element.147) | copy-start | bytes 196612
  383.4 24.2 %collective-permute-start.4 = (f32[128,2048]{1,0:T(8,128)}, f32[128,2048]{1,0:T(8,128)}, u32[]{:S(2)}, u32[]{:S(2)}) collective-permute-start(f32[128,2048]{1,0:T(8,128)} %fusion.32), channel_id=1, source_target_pairs={{0,32},{32,0},{16,48},{48,16},{64,96},{96,64},{80,112},{112,80},{1... | collective-permute-start | bytes 3145736 | tf_op jit(solution)/shard_map/ppermute | solution.py:71
  416.2 42.4 %all-to-all-start.1 = ((f32[2,128,16,192]{1,3,0,2:T(8,128)}), f32[2,128,16,192]{1,3,0,2:T(8,128)S(1)}, u32[]{:S(2)}, u32[]{:S(2)}) async-start(f32[2,128,16,192]{1,3,0,2:T(8,128)} %pad_maximum_fusion.1), calls=%async_computation.2 | async-start | bytes 6291456 | tf_op jit(solution)/shard_map/all_to_all | solution.py:232
  421.2 101.8 %all-gather.9.cloned.1.call-start = ((), (), s32[]{:S(2)}) async-start(), calls=%async_computation.6 | async-start | bytes 4456448 | tf_op jit(solution)/shard_map/all_gather | solution.py:242
  467.7 12.1 %copy-start.4 = (f32[512,512]{0,1:T(8,128)S(1)}, f32[512,512]{0,1:T(8,128)}, u32[]{:S(2)}) copy-start(f32[512,512]{0,1:T(8,128)} %copy-done.3) | copy-start | bytes 3145732
  467.7 210.7 %all-gather.11.cloned.1.call-start = ((), (), s32[]{:S(2)}) async-start(), calls=%async_computation.7 | async-start | bytes 8912896 | tf_op jit(solution)/shard_map/all_gather | solution.py:244
  536.7 50.6 %copy-start.23 = (f32[128,128]{1,0:T(8,128)S(1)}, f32[128,128]{1,0:T(8,128)}, u32[]{:S(2)}) copy-start(f32[128,128]{1,0:T(8,128)} %get-tuple-element.149) | copy-start | bytes 196612
  552.6 34.7 %copy-start.56 = (f32[128,128]{1,0:T(8,128)S(1)}, f32[128,128]{1,0:T(8,128)}, u32[]{:S(2)}) copy-start(f32[128,128]{1,0:T(8,128)} %get-tuple-element.151) | copy-start | bytes 196612
  572.2 21.8 %copy-start.25 = (f32[128,256]{1,0:T(8,128)}, f32[128,256]{1,0:T(8,128)S(1)}, u32[]{:S(2)}) copy-start(f32[128,256]{1,0:T(8,128)S(1)} %concatenate.318) | copy-start | bytes 393220
  611.8 54.7 %copy-start.22 = (f32[128,128]{1,0:T(8,128)S(1)}, f32[128,128]{1,0:T(8,128)}, u32[]{:S(2)}) copy-start(f32[128,128]{1,0:T(8,128)} %get-tuple-element.157) | copy-start | bytes 196612
  629.8 19.4 %copy-start.54 = (f32[128,128]{1,0:T(8,128)}, f32[128,128]{1,0:T(8,128)S(1)}, u32[]{:S(2)}) copy-start(f32[128,128]{1,0:T(8,128)S(1)} %convolution_negate_fusion.7) | copy-start | bytes 196612
  667.5 8.9 %copy-start.46 = (f32[256,256]{1,0:T(8,128)}, f32[256,256]{1,0:T(8,128)S(1)}, u32[]{:S(2)}) copy-start(f32[256,256]{1,0:T(8,128)S(1)} %select_maximum_fusion.10) | copy-start | bytes 786436
  (91 other events, 282.7 us)
Sparse Core Ops, SparseCore 0:
  35.0 110.4 reduce-scatter.1
  164.8 51.8 all-gather.4
  219.4 70.5 all-gather.6
  467.8 55.0 all-gather.8
  524.9 70.4 all-gather.10

commit v6 on v5

--- a/solution.py
+++ b/solution.py
@@ -208,10 +208,8 @@
     gram_blocks = lax.fori_loop(
         0, row_count // step_rows, add_rows, jnp.zeros((target_total, BLK, BLK), jnp.float32)
     )
-    per_front = gram_blocks.reshape(front_total, S, BLK)
-    obs_share = lax.psum_scatter(per_front, "inner", scatter_dimension=1, tiled=True)
-    for bit in range(group_count.bit_length() - 1):
-        obs_share = obs_share + partner_2(obs_share, "outer", bit)
+    gram_parts = gram_blocks.reshape(front_total, inner_count, sep_rows, BLK).transpose(1, 0, 2, 3)
+    gram_parts = gram_parts.reshape(inner_count, -1)
     current = child_update[0]
     pivot_list = []
     border_list = []
@@ -229,7 +227,21 @@
                 owner_major(parent_columns(sibling, sib_map, parent_count), inner_count),
             ]
         )
-        arrived = lax.all_to_all(outgoing, "inner", split_axis=2, concat_axis=1, tiled=True)
+        if level_index == 0:
+            front_parts = outgoing.transpose(2, 0, 1, 3).reshape(inner_count, -1)
+            front_size = front_parts.shape[1]
+            both = lax.all_to_all(
+                jnp.concatenate([front_parts, gram_parts], axis=1), "inner", 0, 0, tiled=True
+            )
+            arrived = both[:, :front_size].reshape(inner_count, 2, B // inner_count, 1, outgoing.shape[3])
+            arrived = arrived.transpose(1, 0, 2, 3, 4).reshape(2, B, 1, outgoing.shape[3])
+            obs_share = jnp.sum(
+                both[:, front_size:].reshape(inner_count, front_total, sep_rows, BLK), axis=0
+            )
+            for bit in range(group_count.bit_length() - 1):
+                obs_share = obs_share + partner_2(obs_share, "outer", bit)
+        else:
+            arrived = lax.all_to_all(outgoing, "inner", split_axis=2, concat_axis=1, tiled=True)
         own_cols = parent_rows(arrived[0, :, 0, :], own_map, parent_count)
         sib_cols = parent_rows(arrived[1, :, 0, :], sib_map, parent_count)
         front_rows = (own_cols + sib_cols).T

time: 714 us -> 769 us (1.077)
  waiting for transfers between devices: 221 us -> 136 us
  blocking collectives: 0 us -> 79.1 us
  local copies, waits for them, and re-layouts: 85.5 us -> 144 us
    reduce_scatter x1 -> x0, waiting for transfers between devices: 82.7 us -> none  [shards(): lax.psum_scatter(per_front, 'inner', scatter_dimension=1, tiled=True)]
    all_to_all x0 -> x1, blocking collectives: none -> 79.1 us  [shards(): lax.all_to_all(jnp.concatenate([front_parts, gram_parts], axis=1), 'inner...]
    reshape x0 -> x8, local copies, waits for them, and re-layouts: none -> 19.6 us  [the longest x2 8.5 us: shards(): both[:, :front_size]]
    all_to_all x0 -> x1, local copies, waits for them, and re-layouts: none -> 18.1 us  [shards(): lax.all_to_all(jnp.concatenate([front_parts, gram_parts], axis=1), 'inner...]
    unnamed x208 -> x206, local copies, waits for them, and re-layouts: 16.3 us -> 20.6 us
    all_to_all x2 -> x1, waiting for transfers between devices: 37.4 us -> 37.4 us  [shards(): lax.all_to_all(outgoing, 'inner', split_axis=2, concat_axis=1, tiled=True)]
  transfers between devices with their start and end apart: 12 -> 10, of which waited for: 8 -> 5; matrix products, arithmetic and copies ran while one was open for 22% -> 26% of each run, Pallas kernels for 28% -> 26%
where the time goes in v6:
time: 769 us; the launch traced here: 756 us
  Pallas kernels  198 us (26%)
  local copies, waits for them, and re-layouts  144 us (19%)
  waiting for transfers between devices  136 us (18%)
  matrix products  115 us (15%)
  blocking collectives  79.1 us (10%)
  other arithmetic  50.4 us (7%)
  between operations  16 us (2%)
  starting transfers between devices  15.9 us (2%)
    pallas_call x16, Pallas kernels, base_cholesky_inverse(): pl.pallas_call(_kernel, out_shape=(jax.ShapeDtypeStruct((n, n), jnp.float...  198 us
    all_gather x2, waiting for transfers between devices, shards(): pivot_all = lax.all_gather(sep_front[:, :S], 'inner', axis=0, tiled=True)  80.5 us
    all_to_all x1, blocking collectives, shards(): lax.all_to_all(jnp.concatenate([front_parts, gram_parts], axis=1), 'inner...  79.1 us
    all_to_all x1, waiting for transfers between devices, shards(): lax.all_to_all(outgoing, 'inner', split_axis=2, concat_axis=1, tiled=True)  37.4 us
    unnamed x206, local copies, waits for them, and re-layouts  20.6 us
    ppermute x5, waiting for transfers between devices, partner_2(): return lax.ppermute(block, axis, route)  18.2 us
    all_to_all x1, local copies, waits for them, and re-layouts, shards(): lax.all_to_all(jnp.concatenate([front_parts, gram_parts], axis=1), 'inner...  18.1 us
    dot_general x12, matrix products, cholesky_inverse(): jnp.dot(lower_21, lower_21.T, precision=HIGH, preferred_element_type=jnp....  17.8 us
  transfers between devices with their start and end apart: 10, of which 5 were waited for; matrix products, arithmetic and copies ran while one was open for 26% of the time, Pallas kernels for 26%

profile of v6, /device:TPU:1, one launch (start us, length us, event | category | flops | bytes accessed | tf_op | source)
XLA Modules:
  0.0 755.6 jit_solution(15384358850955895333)
XLA Ops:
  15.2 25.9 %while.14 = (s32[]{:T(128)}, f32[48,128,128]{2,1,0:T(8,128)S(1)}, s32[2048]{0:T(1024)}, bf16[2048,128]{1,0:T(8,128)(2,1)}, s32[]{:T(128)}, /*index=5*/s32[]{:T(128)}, s32[]{:T(128)}, s32[]{:T(128)}) while((s32[]{:T(128)}, f32[48,128,128]{2,1,0:T(8,128)S(1)}, s32[2048]{0:T(1024)}, bf16[2048,128]{1,0:T(8,128)(2,1)}, s32[]{:T(128)}, ...), condition=%wide.region_5.7_spmd.clone, body=%wide.region_4.6_spmd.clone.sunk | while | flops 405823488 | bytes 6737045 | solution.py:208
  88.6 18.1 %copy.179 = f32[16,1,98304]{2,1,0:T(1,128)S(1)} copy(f32[16,1,98304]{2,0,1:T(8,128)S(1)} %maximum_bitcast_fusion) | data formatting | bytes 12582912 | tf_op jit(solution)/shard_map/all_to_all | solution.py:233
  106.7 79.1 %all_to_all.27 = f32[16,1,98304]{2,1,0:T(1,128)S(1)} all-to-all(f32[16,1,98304]{2,1,0:T(1,128)S(1)} %copy.179), channel_id=1, replica_groups=mesh['outer'=8,'inner'=16] {'inner'}, dimensions={0} | all-to-all | bytes 12582912 | tf_op jit(solution)/shard_map/all_to_all | solution.py:233
  221.6 47.8 %all-gather.5.cloned.1.call-done = f32[1024,1024]{1,0:T(8,128)} async-done(((f32[64,1024]{1,0:T(8,128)}), f32[1024,1024]{1,0:T(8,128)}) %all-gather.5.cloned.1.call-update) | async-done | bytes 4194320 | tf_op jit(solution)/shard_map/all_gather | solution.py:254
  270.8 12.3 %shard_map.67 = (f32[128,128]{1,0:T(8,128)}, f32[128,128]{1,0:T(8,128)}) custom-call(f32[128,128]{1,0:T(8,128)} %slice.318.a_ref), custom_call_target="tpu_custom_call" | custom-call | tf_op jit(solution)/shard_map/pallas_call | solution.py:57
  286.0 12.3 %shard_map.68 = (f32[128,128]{1,0:T(8,128)}, f32[128,128]{1,0:T(8,128)}) custom-call(f32[128,128]{1,0:T(8,128)} %convolution_subtract_fusion.13.a_ref), custom_call_target="tpu_custom_call" | custom-call | tf_op jit(solution)/shard_map/pallas_call | solution.py:57
  303.8 12.5 %shard_map.69 = (f32[128,128]{1,0:T(8,128)}, f32[128,128]{1,0:T(8,128)}) custom-call(f32[128,128]{1,0:T(8,128)} %slice.323.a_ref), custom_call_target="tpu_custom_call" | custom-call | tf_op jit(solution)/shard_map/pallas_call | solution.py:57
  318.3 12.3 %shard_map.70 = (f32[128,128]{1,0:T(8,128)}, f32[128,128]{1,0:T(8,128)}) custom-call(f32[128,128]{1,0:T(8,128)} %convolution_subtract_fusion.12.a_ref), custom_call_target="tpu_custom_call" | custom-call | tf_op jit(solution)/shard_map/pallas_call | solution.py:57
  343.4 12.7 %shard_map.71 = (f32[128,128]{1,0:T(8,128)}, f32[128,128]{1,0:T(8,128)}) custom-call(f32[128,128]{1,0:T(8,128)} %slice.328.a_ref), custom_call_target="tpu_custom_call" | custom-call | tf_op jit(solution)/shard_map/pallas_call | solution.py:57
  359.5 12.3 %shard_map.72 = (f32[128,128]{1,0:T(8,128)}, f32[128,128]{1,0:T(8,128)}) custom-call(f32[128,128]{1,0:T(8,128)} %convolution_subtract_fusion.11.a_ref), custom_call_target="tpu_custom_call" | custom-call | tf_op jit(solution)/shard_map/pallas_call | solution.py:57
  378.7 12.5 %shard_map.73 = (f32[128,128]{1,0:T(8,128)}, f32[128,128]{1,0:T(8,128)}) custom-call(f32[128,128]{1,0:T(8,128)} %slice.333.a_ref), custom_call_target="tpu_custom_call" | custom-call | tf_op jit(solution)/shard_map/pallas_call | solution.py:57
  396.1 12.3 %shard_map.74 = (f32[128,128]{1,0:T(8,128)}, f32[128,128]{1,0:T(8,128)}) custom-call(f32[128,128]{1,0:T(8,128)} %convolution_subtract_fusion.10.a_ref), custom_call_target="tpu_custom_call" | custom-call | tf_op jit(solution)/shard_map/pallas_call | solution.py:57
  418.7 5.8 fusion.12
  444.1 16.2 %collective-permute-done.4 = f32[128,2048]{1,0:T(8,128)} collective-permute-done((f32[128,2048]{1,0:T(8,128)}, f32[128,2048]{1,0:T(8,128)}, u32[]{:S(2)}, u32[]{:S(2)}) %collective-permute-start.4) | collective-permute-done | bytes 1048608 | tf_op jit(solution)/shard_map/ppermute | solution.py:71
  473.9 37.4 %all-to-all-done.1 = f32[2,128,16,192]{1,3,0,2:T(8,128)S(1)} async-done(((f32[2,128,16,192]{1,3,0,2:T(8,128)}), f32[2,128,16,192]{1,3,0,2:T(8,128)S(1)}, u32[]{:S(2)}, u32[]{:S(2)}) %all-to-all-start.1) | async-done | bytes 3145760 | tf_op jit(solution)/shard_map/all_to_all | solution.py:244
  542.9 32.7 %all-gather.9.cloned.1.call-done = f32[1024,1024]{1,0:T(8,128)} async-done(((f32[64,1024]{1,0:T(8,128)}), f32[1024,1024]{1,0:T(8,128)}) %all-gather.9.cloned.1.call-update) | async-done | bytes 4194320 | tf_op jit(solution)/shard_map/all_gather | solution.py:254
  577.0 12.3 %shard_map.75 = (f32[128,128]{1,0:T(8,128)}, f32[128,128]{1,0:T(8,128)}) custom-call(f32[128,128]{1,0:T(8,128)} %slice.348.a_ref), custom_call_target="tpu_custom_call" | custom-call | tf_op jit(solution)/shard_map/pallas_call | solution.py:57
  592.9 12.3 %shard_map.76 = (f32[128,128]{1,0:T(8,128)}, f32[128,128]{1,0:T(8,128)}) custom-call(f32[128,128]{1,0:T(8,128)} %convolution_subtract_fusion.9.a_ref), custom_call_target="tpu_custom_call" | custom-call | tf_op jit(solution)/shard_map/pallas_call | solution.py:57
  611.6 12.3 %shard_map.77 = (f32[128,128]{1,0:T(8,128)}, f32[128,128]{1,0:T(8,128)}) custom-call(f32[128,128]{1,0:T(8,128)} %slice.353.a_ref), custom_call_target="tpu_custom_call" | custom-call | tf_op jit(solution)/shard_map/pallas_call | solution.py:57
  627.6 12.3 %shard_map.78 = (f32[128,128]{1,0:T(8,128)}, f32[128,128]{1,0:T(8,128)}) custom-call(f32[128,128]{1,0:T(8,128)} %convolution_subtract_fusion.8.a_ref), custom_call_target="tpu_custom_call" | custom-call | tf_op jit(solution)/shard_map/pallas_call | solution.py:57
  652.0 12.3 %shard_map.79 = (f32[128,128]{1,0:T(8,128)}, f32[128,128]{1,0:T(8,128)}) custom-call(f32[128,128]{1,0:T(8,128)} %slice.358.a_ref), custom_call_target="tpu_custom_call" | custom-call | tf_op jit(solution)/shard_map/pallas_call | solution.py:57
  667.9 12.3 %shard_map.80 = (f32[128,128]{1,0:T(8,128)}, f32[128,128]{1,0:T(8,128)}) custom-call(f32[128,128]{1,0:T(8,128)} %convolution_subtract_fusion.7.a_ref), custom_call_target="tpu_custom_call" | custom-call | tf_op jit(solution)/shard_map/pallas_call | solution.py:57
  689.0 12.7 %shard_map.81 = (f32[128,128]{1,0:T(8,128)}, f32[128,128]{1,0:T(8,128)}) custom-call(f32[128,128]{1,0:T(8,128)} %slice.363.a_ref), custom_call_target="tpu_custom_call" | custom-call | tf_op jit(solution)/shard_map/pallas_call | solution.py:57
  706.8 12.3 %shard_map.82 = (f32[128,128]{1,0:T(8,128)}, f32[128,128]{1,0:T(8,128)}) custom-call(f32[128,128]{1,0:T(8,128)} %convolution_subtract_fusion.6.a_ref), custom_call_target="tpu_custom_call" | custom-call | tf_op jit(solution)/shard_map/pallas_call | solution.py:57
  (460 shorter events, 304.1 us)
Async XLA Ops:
  7.2 262.2 %all-gather.5.cloned.1.call-start = ((), (), s32[]{:S(2)}) async-start(), calls=%async_computation.2 | async-start | bytes 4456448 | tf_op jit(solution)/shard_map/all_gather | solution.py:254
  9.7 53.9 %collective-permute-start = (f32[128,2048]{0,1:T(8,128)}, f32[128,2048]{0,1:T(8,128)}, u32[]{:S(2)}, u32[]{:S(2)}) collective-permute-start(f32[128,2048]{0,1:T(8,128)} %bitcast.8), channel_id=1, source_target_pairs={{0,16},{16,0},{32,48},{48,32},{64,80},{80,64},{96,112},{112,96},{1... | collective-permute-start | bytes 3145736 | tf_op jit(solution)/shard_map/ppermute | solution.py:71
  11.8 51.1 %copy-start.94 = (s32[16]{0:T(128)}, s32[16]{0:T(128)S(1)}, u32[]{:S(2)}) copy-start(s32[16]{0:T(128)S(1)} %get-tuple-element.215) | copy-start | bytes 196
  12.5 31.7 %copy-start.91 = (pred[24]{0:T(512)(128)(4,1)}, pred[24]{0:T(512)(128)(4,1)S(1)}, u32[]{:S(2)}) copy-start(pred[24]{0:T(512)(128)(4,1)S(1)} %compare_and_fusion.2) | copy-start | bytes 76
  12.6 31.6 %copy-start.86 = (pred[24]{0:T(512)(128)(4,1)}, pred[24]{0:T(512)(128)(4,1)S(1)}, u32[]{:S(2)}) copy-start(pred[24]{0:T(512)(128)(4,1)S(1)} %get-tuple-element.223) | copy-start | bytes 76
  190.1 10.9 %collective-permute-start.1 = (f32[6,64,128]{2,1,0:T(8,128)S(1)}, f32[6,64,128]{2,1,0:T(8,128)}, u32[]{:S(2)}, u32[]{:S(2)}) collective-permute-start(f32[6,64,128]{2,1,0:T(8,128)S(1)} %bitcast.233), channel_id=1, source_target_pairs={{0,16},{16,0},{32,48},{48,32},{64,80},{80,64},{96,112},{112,96},{1... | collective-permute-start | bytes 589832 | tf_op jit(solution)/shard_map/ppermute | solution.py:71
  202.0 8.1 %collective-permute-start.2 = (f32[6,64,128]{2,1,0:T(8,128)S(1)}, f32[6,64,128]{2,1,0:T(8,128)S(1)}, u32[]{:S(2)}, u32[]{:S(2)}) collective-permute-start(f32[6,64,128]{2,1,0:T(8,128)S(1)} %add.170), channel_id=1, source_target_pairs={{0,32},{32,0},{16,48},{48,16},{64,96},{96,64},{80,112},{112,80},{1... | collective-permute-start | bytes 589832 | tf_op jit(solution)/shard_map/ppermute | solution.py:71
  210.1 8.3 %collective-permute-start.3 = (f32[6,64,128]{2,1,0:T(8,128)S(1)}, f32[6,64,128]{2,1,0:T(8,128)S(1)}, u32[]{:S(2)}, u32[]{:S(2)}) collective-permute-start(f32[6,64,128]{2,1,0:T(8,128)S(1)} %add.171), channel_id=1, source_target_pairs={{0,64},{64,0},{16,80},{80,16},{32,96},{96,32},{48,112},{112,48},{1... | collective-permute-start | bytes 589832 | tf_op jit(solution)/shard_map/ppermute | solution.py:71
  219.8 198.9 %all-gather.7.cloned.1.call-start = ((), (), s32[]{:S(2)}) async-start(), calls=%async_computation.3 | async-start | bytes 8912896 | tf_op jit(solution)/shard_map/all_gather | solution.py:256
  283.1 48.3 %copy-start.24 = (f32[128,128]{1,0:T(8,128)S(1)}, f32[128,128]{1,0:T(8,128)}, u32[]{:S(2)}) copy-start(f32[128,128]{1,0:T(8,128)} %get-tuple-element.133) | copy-start | bytes 196612
  298.3 36.3 %copy-start.57 = (f32[128,128]{1,0:T(8,128)S(1)}, f32[128,128]{1,0:T(8,128)}, u32[]{:S(2)}) copy-start(f32[128,128]{1,0:T(8,128)} %get-tuple-element.135) | copy-start | bytes 196612
  301.7 33.2 %copy-start.4 = (f32[256,256]{0,1:T(8,128)}, f32[256,256]{0,1:T(8,128)S(1)}, u32[]{:S(2)}) copy-start(f32[256,256]{0,1:T(8,128)S(1)} %fusion.71) | copy-start | bytes 786436
  339.1 75.2 %copy-start.2 = (f32[512,512]{0,1:T(8,128)}, f32[512,512]{0,1:T(8,128)S(1)}, u32[]{:S(2)}) copy-start(f32[512,512]{0,1:T(8,128)S(1)} %fusion.41) | copy-start | bytes 3145732
  436.1 24.2 %collective-permute-start.4 = (f32[128,2048]{1,0:T(8,128)}, f32[128,2048]{1,0:T(8,128)}, u32[]{:S(2)}, u32[]{:S(2)}) collective-permute-start(f32[128,2048]{1,0:T(8,128)} %fusion.32), channel_id=1, source_target_pairs={{0,32},{32,0},{16,48},{48,16},{64,96},{96,64},{80,112},{112,80},{1... | collective-permute-start | bytes 3145736 | tf_op jit(solution)/shard_map/ppermute | solution.py:71
  468.9 42.5 %all-to-all-start.1 = ((f32[2,128,16,192]{1,3,0,2:T(8,128)}), f32[2,128,16,192]{1,3,0,2:T(8,128)S(1)}, u32[]{:S(2)}, u32[]{:S(2)}) async-start(f32[2,128,16,192]{1,3,0,2:T(8,128)} %pad_maximum_fusion), calls=%async_computation.1 | async-start | bytes 6291456 | tf_op jit(solution)/shard_map/all_to_all | solution.py:244
  473.8 101.7 %all-gather.9.cloned.1.call-start = ((), (), s32[]{:S(2)}) async-start(), calls=%async_computation.4 | async-start | bytes 4456448 | tf_op jit(solution)/shard_map/all_gather | solution.py:254
  520.5 12.1 %copy-start.3 = (f32[512,512]{0,1:T(8,128)S(1)}, f32[512,512]{0,1:T(8,128)}, u32[]{:S(2)}) copy-start(f32[512,512]{0,1:T(8,128)} %copy-done.2) | copy-start | bytes 3145732
  520.5 210.5 %all-gather.11.cloned.1.call-start = ((), (), s32[]{:S(2)}) async-start(), calls=%async_computation.5 | async-start | bytes 8912896 | tf_op jit(solution)/shard_map/all_gather | solution.py:256
  589.3 50.5 %copy-start.23 = (f32[128,128]{1,0:T(8,128)S(1)}, f32[128,128]{1,0:T(8,128)}, u32[]{:S(2)}) copy-start(f32[128,128]{1,0:T(8,128)} %get-tuple-element.149) | copy-start | bytes 196612
  605.2 34.7 %copy-start.56 = (f32[128,128]{1,0:T(8,128)S(1)}, f32[128,128]{1,0:T(8,128)}, u32[]{:S(2)}) copy-start(f32[128,128]{1,0:T(8,128)} %get-tuple-element.151) | copy-start | bytes 196612
  624.8 21.8 %copy-start.25 = (f32[128,256]{1,0:T(8,128)}, f32[128,256]{1,0:T(8,128)S(1)}, u32[]{:S(2)}) copy-start(f32[128,256]{1,0:T(8,128)S(1)} %concatenate.322) | copy-start | bytes 393220
  664.3 54.8 %copy-start.22 = (f32[128,128]{1,0:T(8,128)S(1)}, f32[128,128]{1,0:T(8,128)}, u32[]{:S(2)}) copy-start(f32[128,128]{1,0:T(8,128)} %get-tuple-element.157) | copy-start | bytes 196612
  682.3 19.4 %copy-start.54 = (f32[128,128]{1,0:T(8,128)}, f32[128,128]{1,0:T(8,128)S(1)}, u32[]{:S(2)}) copy-start(f32[128,128]{1,0:T(8,128)S(1)} %convolution_negate_fusion.7) | copy-start | bytes 196612
  720.0 8.9 %copy-start.46 = (f32[256,256]{1,0:T(8,128)}, f32[256,256]{1,0:T(8,128)S(1)}, u32[]{:S(2)}) copy-start(f32[256,256]{1,0:T(8,128)S(1)} %select_maximum_fusion.10) | copy-start | bytes 786436
  (87 other events, 278.9 us)
Sparse Core Ops, SparseCore 0:
  219.9 49.3 all-gather.4
  272.1 70.5 all-gather.6
  520.6 54.9 all-gather.8
  577.6 70.4 all-gather.10

commit v7 on v5

--- a/solution.py
+++ b/solution.py
@@ -257,8 +257,24 @@
             precision=HIGH,
             preferred_element_type=jnp.float32,
         )
-        zero = jnp.zeros((half, half), jnp.float32)
-        pivot_lower = jnp.block([[lower_11, zero], [lower_21, lower_22]])
+        top_count = half // sep_rows
+        top_start = jnp.minimum(member, top_count - 1) * sep_rows
+        low_start = jnp.maximum(member - top_count, 0) * sep_rows
+        top_rows = jnp.concatenate(
+            [
+                lax.dynamic_slice_in_dim(lower_11, top_start, sep_rows, 0),
+                jnp.zeros((sep_rows, half), jnp.float32),
+            ],
+            axis=1,
+        )
+        low_rows = jnp.concatenate(
+            [
+                lax.dynamic_slice_in_dim(lower_21, low_start, sep_rows, 0),
+                lax.dynamic_slice_in_dim(lower_22, low_start, sep_rows, 0),
+            ],
+            axis=1,
+        )
+        pivot_rows = jnp.where(member < top_count, top_rows, low_rows)
         border_left = jnp.dot(
             coupling_all[:, :half], inverse_11.T, precision=HIGH, preferred_element_type=jnp.float32
         )
@@ -277,7 +293,7 @@
             "rs,cs->rc", own_right, border_right, precision=HIGH, preferred_element_type=jnp.float32
         )
         current = border_front[:, S:] - product
-        pivot_list.append(lax.dynamic_slice_in_dim(pivot_lower, member * sep_rows, sep_rows, 0))
+        pivot_list.append(pivot_rows)
         border_list.append(border_factor)
     pivot_factor = jnp.stack(pivot_list)[:, None]
     border_out = jnp.stack(border_list)[:, None]

time: 714 us -> 701 us (0.982)
  other arithmetic: 43.7 us -> 34.6 us
  waiting for transfers between devices: 221 us -> 230 us
    all_gather x2, waiting for transfers between devices: 82.7 us -> 91.2 us  [shards(): pivot_all = lax.all_gather(sep_front[:, :S], 'inner', axis=0, tiled=True)]
    concatenate x10 -> x7, other arithmetic: 15.2 us -> 8.21 us  [cholesky_inverse(): lower = jnp.block([[lower_11, zero], [lower_21, lower_22]])]
    unnamed x208 -> x182, local copies, waits for them, and re-layouts: 16.3 us -> 13.7 us
  transfers between devices with their start and end apart: 12 -> 12, of which waited for: 8 -> 8; matrix products, arithmetic and copies ran while one was open for 22% -> 20% of each run, Pallas kernels for 28% -> 29%
where the time goes in v7:
time: 701 us; the launch traced here: 691 us
  waiting for transfers between devices  230 us (33%)
  Pallas kernels  198 us (28%)
  matrix products  111 us (16%)
  local copies, waits for them, and re-layouts  78.4 us (11%)
  other arithmetic  34.6 us (5%)
  starting transfers between devices  22.2 us (3%)
  between operations  16 us (2%)
    pallas_call x16, Pallas kernels, base_cholesky_inverse(): pl.pallas_call(_kernel, out_shape=(jax.ShapeDtypeStruct((n, n), jnp.float...  198 us
    all_gather x2, waiting for transfers between devices, shards(): pivot_all = lax.all_gather(sep_front[:, :S], 'inner', axis=0, tiled=True)  91.2 us
    reduce_scatter x1, waiting for transfers between devices, shards(): lax.psum_scatter(per_front, 'inner', scatter_dimension=1, tiled=True)  82.7 us
    all_to_all x2, waiting for transfers between devices, shards(): lax.all_to_all(outgoing, 'inner', split_axis=2, concat_axis=1, tiled=True)  37.4 us
    ppermute x5, waiting for transfers between devices, partner_2(): return lax.ppermute(block, axis, route)  18.6 us
    dot_general x12, matrix products, cholesky_inverse(): jnp.dot(lower_21, lower_21.T, precision=HIGH, preferred_element_type=jnp....  15.8 us
  transfers between devices with their start and end apart: 12, of which 8 were waited for; matrix products, arithmetic and copies ran while one was open for 20% of the time, Pallas kernels for 29%

profile of v7, /device:TPU:1, one launch (start us, length us, event | category | flops | bytes accessed | tf_op | source)
XLA Modules:
  0.0 690.7 jit_solution(17556801177536698527)
XLA Ops:
  7.2 25.9 %while.14 = (s32[]{:T(128)}, f32[48,128,128]{2,1,0:T(8,128)S(1)}, s32[2048]{0:T(1024)}, bf16[2048,128]{1,0:T(8,128)(2,1)}, s32[]{:T(128)}, /*index=5*/s32[]{:T(128)}, s32[]{:T(128)}, s32[]{:T(128)}) while((s32[]{:T(128)}, f32[48,128,128]{2,1,0:T(8,128)S(1)}, s32[2048]{0:T(1024)}, bf16[2048,128]{1,0:T(8,128)(2,1)}, s32[]{:T(128)}, ...), condition=%wide.region_5.8_spmd.clone, body=%wide.region_4.7_spmd.clone.sunk | while | flops 405823488 | bytes 6737053 | solution.py:208
  55.8 6.9 all-to-all-start
  62.7 82.7 %reduce-scatter.2.cloned.1.call-done = f32[6,64,128]{2,1,0:T(8,128)} async-done(((f32[6,1024,128]{2,1,0:T(8,128)}), f32[6,64,128]{2,1,0:T(8,128)}) %reduce-scatter.2.cloned.1.call-update) | async-done | bytes 196624 | tf_op jit(solution)/shard_map/reduce_scatter | solution.py:212
  167.0 49.5 %all-gather.5.cloned.1.call-done = f32[1024,1024]{1,0:T(8,128)} async-done(((f32[64,1024]{1,0:T(8,128)}), f32[1024,1024]{1,0:T(8,128)}) %all-gather.5.cloned.1.call-update) | async-done | bytes 4194320 | tf_op jit(solution)/shard_map/all_gather | solution.py:242
  218.0 12.3 %shard_map.67 = (f32[128,128]{1,0:T(8,128)}, f32[128,128]{1,0:T(8,128)}) custom-call(f32[128,128]{1,0:T(8,128)} %slice.308.a_ref), custom_call_target="tpu_custom_call" | custom-call | tf_op jit(solution)/shard_map/pallas_call | solution.py:57
  233.2 12.3 %shard_map.68 = (f32[128,128]{1,0:T(8,128)}, f32[128,128]{1,0:T(8,128)}) custom-call(f32[128,128]{1,0:T(8,128)} %convolution_subtract_fusion.13.a_ref), custom_call_target="tpu_custom_call" | custom-call | tf_op jit(solution)/shard_map/pallas_call | solution.py:57
  250.9 12.5 %shard_map.69 = (f32[128,128]{1,0:T(8,128)}, f32[128,128]{1,0:T(8,128)}) custom-call(f32[128,128]{1,0:T(8,128)} %slice.313.a_ref), custom_call_target="tpu_custom_call" | custom-call | tf_op jit(solution)/shard_map/pallas_call | solution.py:57
  266.2 12.3 %shard_map.70 = (f32[128,128]{1,0:T(8,128)}, f32[128,128]{1,0:T(8,128)}) custom-call(f32[128,128]{1,0:T(8,128)} %convolution_subtract_fusion.12.a_ref), custom_call_target="tpu_custom_call" | custom-call | tf_op jit(solution)/shard_map/pallas_call | solution.py:57
  290.3 12.7 %shard_map.71 = (f32[128,128]{1,0:T(8,128)}, f32[128,128]{1,0:T(8,128)}) custom-call(f32[128,128]{1,0:T(8,128)} %slice.318.a_ref), custom_call_target="tpu_custom_call" | custom-call | tf_op jit(solution)/shard_map/pallas_call | solution.py:57
  305.9 12.3 %shard_map.72 = (f32[128,128]{1,0:T(8,128)}, f32[128,128]{1,0:T(8,128)}) custom-call(f32[128,128]{1,0:T(8,128)} %convolution_subtract_fusion.11.a_ref), custom_call_target="tpu_custom_call" | custom-call | tf_op jit(solution)/shard_map/pallas_call | solution.py:57
  324.4 12.3 %shard_map.73 = (f32[128,128]{1,0:T(8,128)}, f32[128,128]{1,0:T(8,128)}) custom-call(f32[128,128]{1,0:T(8,128)} %slice.323.a_ref), custom_call_target="tpu_custom_call" | custom-call | tf_op jit(solution)/shard_map/pallas_call | solution.py:57
  340.6 12.3 %shard_map.74 = (f32[128,128]{1,0:T(8,128)}, f32[128,128]{1,0:T(8,128)}) custom-call(f32[128,128]{1,0:T(8,128)} %convolution_subtract_fusion.10.a_ref), custom_call_target="tpu_custom_call" | custom-call | tf_op jit(solution)/shard_map/pallas_call | solution.py:57
  386.4 16.2 %collective-permute-done.4 = f32[128,2048]{1,0:T(8,128)} collective-permute-done((f32[128,2048]{1,0:T(8,128)}, f32[128,2048]{1,0:T(8,128)}, u32[]{:S(2)}, u32[]{:S(2)}) %collective-permute-start.4) | collective-permute-done | bytes 1048608 | tf_op jit(solution)/shard_map/ppermute | solution.py:71
  416.1 37.4 %all-to-all-done.1 = f32[2,128,16,192]{1,3,0,2:T(8,128)S(1)} async-done(((f32[2,128,16,192]{1,3,0,2:T(8,128)}), f32[2,128,16,192]{1,3,0,2:T(8,128)S(1)}, u32[]{:S(2)}, u32[]{:S(2)}) %all-to-all-start.1) | async-done | bytes 3145760 | tf_op jit(solution)/shard_map/all_to_all | solution.py:232
  476.2 41.7 %all-gather.9.cloned.1.call-done = f32[1024,1024]{1,0:T(8,128)} async-done(((f32[64,1024]{1,0:T(8,128)}), f32[1024,1024]{1,0:T(8,128)}) %all-gather.9.cloned.1.call-update) | async-done | bytes 4194320 | tf_op jit(solution)/shard_map/all_gather | solution.py:242
  519.4 12.3 %shard_map.75 = (f32[128,128]{1,0:T(8,128)}, f32[128,128]{1,0:T(8,128)}) custom-call(f32[128,128]{1,0:T(8,128)} %slice.338.a_ref), custom_call_target="tpu_custom_call" | custom-call | tf_op jit(solution)/shard_map/pallas_call | solution.py:57
  535.2 12.3 %shard_map.76 = (f32[128,128]{1,0:T(8,128)}, f32[128,128]{1,0:T(8,128)}) custom-call(f32[128,128]{1,0:T(8,128)} %convolution_subtract_fusion.9.a_ref), custom_call_target="tpu_custom_call" | custom-call | tf_op jit(solution)/shard_map/pallas_call | solution.py:57
  553.8 12.5 %shard_map.77 = (f32[128,128]{1,0:T(8,128)}, f32[128,128]{1,0:T(8,128)}) custom-call(f32[128,128]{1,0:T(8,128)} %slice.343.a_ref), custom_call_target="tpu_custom_call" | custom-call | tf_op jit(solution)/shard_map/pallas_call | solution.py:57
  569.9 12.3 %shard_map.78 = (f32[128,128]{1,0:T(8,128)}, f32[128,128]{1,0:T(8,128)}) custom-call(f32[128,128]{1,0:T(8,128)} %convolution_subtract_fusion.8.a_ref), custom_call_target="tpu_custom_call" | custom-call | tf_op jit(solution)/shard_map/pallas_call | solution.py:57
  592.8 12.5 %shard_map.79 = (f32[128,128]{1,0:T(8,128)}, f32[128,128]{1,0:T(8,128)}) custom-call(f32[128,128]{1,0:T(8,128)} %slice.348.a_ref), custom_call_target="tpu_custom_call" | custom-call | tf_op jit(solution)/shard_map/pallas_call | solution.py:57
  608.0 12.3 %shard_map.80 = (f32[128,128]{1,0:T(8,128)}, f32[128,128]{1,0:T(8,128)}) custom-call(f32[128,128]{1,0:T(8,128)} %convolution_subtract_fusion.7.a_ref), custom_call_target="tpu_custom_call" | custom-call | tf_op jit(solution)/shard_map/pallas_call | solution.py:57
  627.3 12.7 %shard_map.81 = (f32[128,128]{1,0:T(8,128)}, f32[128,128]{1,0:T(8,128)}) custom-call(f32[128,128]{1,0:T(8,128)} %slice.353.a_ref), custom_call_target="tpu_custom_call" | custom-call | tf_op jit(solution)/shard_map/pallas_call | solution.py:57
  643.5 12.3 %shard_map.82 = (f32[128,128]{1,0:T(8,128)}, f32[128,128]{1,0:T(8,128)}) custom-call(f32[128,128]{1,0:T(8,128)} %convolution_subtract_fusion.6.a_ref), custom_call_target="tpu_custom_call" | custom-call | tf_op jit(solution)/shard_map/pallas_call | solution.py:57
  666.2 5.6 fusion.16
  (428 shorter events, 236.1 us)
Async XLA Ops:
  7.2 138.2 %reduce-scatter.2.cloned.1.call-start = ((), (), s32[]{:S(2)}) async-start(), calls=%async_computation.3 | async-start | bytes 3342336 | tf_op jit(solution)/shard_map/reduce_scatter | solution.py:212
  37.4 9.5 %collective-permute-start = (f32[128,2048]{0,1:T(8,128)}, f32[128,2048]{0,1:T(8,128)}, u32[]{:S(2)}, u32[]{:S(2)}) collective-permute-start(f32[128,2048]{0,1:T(8,128)} %bitcast.8), channel_id=1, source_target_pairs={{0,16},{16,0},{32,48},{48,32},{64,80},{80,64},{96,112},{112,96},{1... | collective-permute-start | bytes 3145736 | tf_op jit(solution)/shard_map/ppermute | solution.py:71
  55.8 91.9 %all-to-all-start = ((f32[2,128,16,192]{1,3,0,2:T(8,128)}), f32[2,128,16,192]{1,3,0,2:T(8,128)S(1)}, u32[]{:S(2)}, u32[]{:S(2)}) async-start(f32[2,128,16,192]{1,3,0,2:T(8,128)} %pad_maximum_fusion), calls=%async_computation | async-start | bytes 6291456 | tf_op jit(solution)/shard_map/all_to_all | solution.py:232
  62.6 153.9 %all-gather.5.cloned.1.call-start = ((), (), s32[]{:S(2)}) async-start(), calls=%async_computation.4 | async-start | bytes 4456448 | tf_op jit(solution)/shard_map/all_gather | solution.py:242
  145.4 3.7 collective-permute-start.1
  150.1 6.2 collective-permute-start.2
  156.2 6.8 collective-permute-start.3
  164.5 197.5 %all-gather.7.cloned.1.call-start = ((), (), s32[]{:S(2)}) async-start(), calls=%async_computation.5 | async-start | bytes 8912896 | tf_op jit(solution)/shard_map/all_gather | solution.py:244
  230.3 48.1 %copy-start.22 = (f32[128,128]{1,0:T(8,128)S(1)}, f32[128,128]{1,0:T(8,128)}, u32[]{:S(2)}) copy-start(f32[128,128]{1,0:T(8,128)} %get-tuple-element.133) | copy-start | bytes 196612
  245.5 36.0 %copy-start.46 = (f32[128,128]{1,0:T(8,128)S(1)}, f32[128,128]{1,0:T(8,128)}, u32[]{:S(2)}) copy-start(f32[128,128]{1,0:T(8,128)} %get-tuple-element.135) | copy-start | bytes 196612
  303.0 49.9 %copy-start.21 = (f32[128,128]{1,0:T(8,128)S(1)}, f32[128,128]{1,0:T(8,128)}, u32[]{:S(2)}) copy-start(f32[128,128]{1,0:T(8,128)} %get-tuple-element.141) | copy-start | bytes 196612
  318.2 37.8 %copy-start.45 = (f32[128,128]{1,0:T(8,128)S(1)}, f32[128,128]{1,0:T(8,128)}, u32[]{:S(2)}) copy-start(f32[128,128]{1,0:T(8,128)} %get-tuple-element.143) | copy-start | bytes 196612
  321.6 38.4 %copy-start.3 = (f32[256,256]{0,1:T(8,128)}, f32[256,256]{0,1:T(8,128)S(1)}, u32[]{:S(2)}) copy-start(f32[256,256]{0,1:T(8,128)S(1)} %fusion.43) | copy-start | bytes 786436
  378.4 24.2 %collective-permute-start.4 = (f32[128,2048]{1,0:T(8,128)}, f32[128,2048]{1,0:T(8,128)}, u32[]{:S(2)}, u32[]{:S(2)}) collective-permute-start(f32[128,2048]{1,0:T(8,128)} %fusion.30), channel_id=1, source_target_pairs={{0,32},{32,0},{16,48},{48,16},{64,96},{96,64},{80,112},{112,80},{1... | collective-permute-start | bytes 3145736 | tf_op jit(solution)/shard_map/ppermute | solution.py:71
  411.1 42.4 %all-to-all-start.1 = ((f32[2,128,16,192]{1,3,0,2:T(8,128)}), f32[2,128,16,192]{1,3,0,2:T(8,128)S(1)}, u32[]{:S(2)}, u32[]{:S(2)}) async-start(f32[2,128,16,192]{1,3,0,2:T(8,128)} %pad_maximum_fusion.1), calls=%async_computation.2 | async-start | bytes 6291456 | tf_op jit(solution)/shard_map/all_to_all | solution.py:232
  416.1 101.8 %all-gather.9.cloned.1.call-start = ((), (), s32[]{:S(2)}) async-start(), calls=%async_computation.6 | async-start | bytes 4456448 | tf_op jit(solution)/shard_map/all_gather | solution.py:242
  462.7 203.4 %all-gather.11.cloned.1.call-start = ((), (), s32[]{:S(2)}) async-start(), calls=%async_computation.7 | async-start | bytes 8912896 | tf_op jit(solution)/shard_map/all_gather | solution.py:244
  531.7 50.5 %copy-start.20 = (f32[128,128]{1,0:T(8,128)S(1)}, f32[128,128]{1,0:T(8,128)}, u32[]{:S(2)}) copy-start(f32[128,128]{1,0:T(8,128)} %get-tuple-element.149) | copy-start | bytes 196612
  547.6 34.6 %copy-start.44 = (f32[128,128]{1,0:T(8,128)S(1)}, f32[128,128]{1,0:T(8,128)}, u32[]{:S(2)}) copy-start(f32[128,128]{1,0:T(8,128)} %get-tuple-element.151) | copy-start | bytes 196612
  592.2 29.3 %copy-start.10 = (f32[512,512]{1,0:T(8,128)}, f32[512,512]{1,0:T(8,128)S(1)}, u32[]{:S(2)}) copy-start(f32[512,512]{1,0:T(8,128)S(1)} %convolution_subtract_fusion) | copy-start | bytes 3145732
  605.3 53.2 %copy-start.19 = (f32[128,128]{1,0:T(8,128)S(1)}, f32[128,128]{1,0:T(8,128)}, u32[]{:S(2)}) copy-start(f32[128,128]{1,0:T(8,128)} %get-tuple-element.157) | copy-start | bytes 196612
  623.1 35.5 %copy-start.39 = (f32[128,128]{1,0:T(8,128)S(1)}, f32[128,128]{1,0:T(8,128)}, u32[]{:S(2)}) copy-start(f32[128,128]{1,0:T(8,128)} %get-tuple-element.159) | copy-start | bytes 196612
  623.1 36.6 %copy-start.30 = (f32[256,256]{1,0:T(8,128)S(1)}, f32[256,256]{1,0:T(8,128)}, u32[]{:S(2)}) copy-start(f32[256,256]{1,0:T(8,128)} %select_maximum_fusion.15) | copy-start | bytes 786436
  624.4 34.1 %copy-start.42 = (f32[128,128]{1,0:T(8,128)S(1)}, f32[128,128]{1,0:T(8,128)}, u32[]{:S(2)}) copy-start(f32[128,128]{1,0:T(8,128)} %copy-done.41) | copy-start | bytes 196612
  (78 other events, 335.9 us)
Sparse Core Ops, SparseCore 0:
  35.0 110.3 reduce-scatter.1
  164.6 51.8 all-gather.4
  219.3 70.4 all-gather.6
  462.9 55.0 all-gather.8
  519.9 70.4 all-gather.10
